TPU v7x, 128 devices: a whole 4x4x4 slice. The times are simulated.
128 devices in a mesh: seq: 32 (over y, z, core), tp: 4 (over x).
Axes of the slice: x: 4, y: 4, z: 4, core: 2. Of those that a mesh axis runs over, the one named last changes fastest.
Arguments:
- rollout_rows: bfloat16 [16384, 8192], P('seq', 'tp'), may hold values from -100 to 100
- plan: int32 [16384], P('seq'), may hold values from 0 to 16383, as said below
- segment_ids: int32 [16384], P('seq'), may hold values from 0 to 256, as said below
- norm_gain: float32 [8192], replicated, may hold values from 0.1 to 1.9
- q_weight: bfloat16 [8192, 4096], P('seq', 'tp'), may hold values from -0.0625 to 0.0625
- k_weight: bfloat16 [8192, 512], P('seq', 'tp'), may hold values from -0.0625 to 0.0625
- v_weight: bfloat16 [8192, 512], P('seq', 'tp'), may hold values from -0.0625 to 0.0625
- q_bias: float32 [4096], P('tp'), may hold values from -40 to 40
- k_bias: float32 [512], P('tp'), may hold values from -40 to 40
- v_bias: float32 [512], P('tp'), may hold values from -3 to 3
Outputs:
- context: bfloat16 [16384, 4096], P('seq', 'tp')
Inputs may be any that keep to these rules, and one draw needn't show every extreme that they name: plan is a permutation of the learner rows; rollout row r goes to learner shard plan[r] // 512. The rows of one device go 16 to every learner shard, except 20 rows to one shard and 12 rows to another. `segment_ids`: within each learner shard the ids start at 0, never fall and rise by one at each new sequence; each sequence has 1 to 256 rows and one sequence of every shard has exactly 256; no sequence crosses a shard.
All inputs are finite; a program needn't handle non-finite values.
Results may differ from a plain program's by a relative error of at most 0.012.
The roundings to bfloat16 on the way count: a program that leaves them out, or rounds other values in their place, can miss the bound.
Values may be sent and summed in bfloat16 or wider, within the bound.
No kernel may reach another device: no remote copies, remote signals or barrier semaphores. Data moves between devices by JAX's collectives and lax.ppermute only.
A program may use at most 128 MiB of HBM per device.

v0:
```python
import math

import jax
import jax.numpy as jnp
from jax import lax
from jax.sharding import PartitionSpec as P

HEAD = 128


EPS = 1e-06
ROPE_BASE = 1000000.0


def rotate(tensor, positions):
    half_size = tensor.shape[-1] // 2
    frequency = jnp.exp(
        jnp.arange(half_size, dtype=jnp.float32) * (-2.0 * math.log(ROPE_BASE) / tensor.shape[-1])
    )
    angles = positions.astype(jnp.float32)[:, None] * frequency[None, :]
    cosine = jnp.cos(angles)[:, None, :]
    sine_part = jnp.sin(angles)[:, None, :]
    front_half = tensor[..., :half_size]
    back_half = tensor[..., half_size:]
    return jnp.concatenate(
        [front_half * cosine - back_half * sine_part, back_half * cosine + front_half * sine_part],
        axis=-1,
    )


def positions_of(segments):
    length = segments.shape[-1]
    counter = jnp.arange(length, dtype=jnp.int32)
    starts = jnp.concatenate([jnp.ones((1,), dtype=bool), segments[1:] != segments[:-1]])
    marked = jnp.where(starts, counter, jnp.zeros_like(counter))
    return counter - lax.cummax(marked, axis=0)


def local(
    rollout_rows, plan, segment_ids, norm_gain, q_weight, k_weight, v_weight, q_bias, k_bias, v_bias
):
    row_count = rollout_rows.shape[0]
    peer_count = lax.axis_size("seq")
    slots_each = row_count // peer_count + row_count // (4 * peer_count)
    slot_total = peer_count * slots_each
    target = plan // row_count
    learner_slot = plan % row_count
    matches = (target[:, None] == jnp.arange(peer_count, dtype=jnp.int32)[None, :]).astype(
        jnp.int32
    )
    ranking = jnp.sum((jnp.cumsum(matches, axis=0) - 1) * matches, axis=1)
    flat_slot = target * slots_each + ranking
    slot_numbers = jnp.arange(slot_total, dtype=jnp.int32)
    row_numbers = jnp.arange(row_count, dtype=jnp.int32)
    slot_hits = flat_slot[None, :] == slot_numbers[:, None]
    filled = jnp.any(slot_hits, axis=1)
    source_index = jnp.sum(jnp.where(slot_hits, row_numbers[None, :], 0), axis=1)
    parcels = jnp.where(filled, jnp.take(learner_slot, source_index, axis=0), row_count).reshape(
        peer_count, slots_each
    )
    full_rows = lax.all_gather(rollout_rows, "tp", axis=1, tiled=True)
    picked = jnp.take(full_rows, source_index, axis=0)
    picked = jnp.where(filled[:, None], picked, jnp.zeros_like(picked))
    arrived = lax.all_to_all(
        picked.reshape(peer_count, slots_each, full_rows.shape[1]),
        "seq",
        split_axis=0,
        concat_axis=0,
        tiled=True,
    )
    labels = lax.all_to_all(parcels, "seq", split_axis=0, concat_axis=0, tiled=True)
    flat_rows = arrived.reshape(slot_total, arrived.shape[2])
    label_hits = labels.reshape(slot_total)[None, :] == row_numbers[:, None]
    slot_of_row = jnp.sum(jnp.where(label_hits, slot_numbers[None, :], 0), axis=1)
    learner_rows = jnp.take(flat_rows, slot_of_row, axis=0)
    widened = learner_rows.astype(jnp.float32)
    mean_sq = jnp.mean(widened * widened, axis=-1, keepdims=True)
    normed = (widened * lax.rsqrt(mean_sq + EPS) * norm_gain).astype(jnp.bfloat16)

    def add_rows(weight_piece):
        return jnp.dot(normed, weight_piece, preferred_element_type=jnp.float32)

    queries = add_rows(lax.all_gather(q_weight, "seq", axis=0, tiled=True))
    key_proj = add_rows(lax.all_gather(k_weight, "seq", axis=0, tiled=True))
    value_proj = add_rows(lax.all_gather(v_weight, "seq", axis=0, tiled=True))
    local_heads = q_weight.shape[1] // HEAD
    local_groups = k_weight.shape[1] // HEAD
    group_size = local_heads // local_groups
    positions = positions_of(segment_ids)
    q_rot = rotate((queries + q_bias).reshape(row_count, local_heads, HEAD), positions).astype(
        jnp.bfloat16
    )
    q_rot = q_rot.reshape(row_count, local_groups, group_size, HEAD)
    k_rot = rotate((key_proj + k_bias).reshape(row_count, local_groups, HEAD), positions).astype(
        jnp.bfloat16
    )
    value_heads = (value_proj + v_bias).astype(jnp.bfloat16).reshape(row_count, local_groups, HEAD)
    block_rows = min(512, row_count)
    row_index = jnp.arange(row_count, dtype=jnp.int32)
    scores = jnp.einsum(
        "qkgd,pkd->kgqp", q_rot, k_rot, preferred_element_type=jnp.float32
    ) / math.sqrt(HEAD)
    allowed = (segment_ids[0:block_rows, None] == segment_ids[None, :block_rows]) & (
        row_index[0:block_rows, None] >= row_index[None, :block_rows]
    )
    scores = jnp.where(allowed[None, None], scores, -jnp.inf)
    highest = jnp.max(scores, axis=-1, keepdims=True)
    expo = jnp.exp(scores - highest)
    probs = (expo / jnp.sum(expo, axis=-1, keepdims=True)).astype(jnp.bfloat16)
    mixed = jnp.einsum("kgqp,pkd->qkgd", probs, value_heads, preferred_element_type=jnp.float32)
    outputs = mixed.astype(jnp.bfloat16).reshape(block_rows, local_heads * HEAD)
    return outputs


def solution(mesh):
    in_specs = (
        P("seq", "tp"),
        P("seq"),
        P("seq"),
        P(),
        P("seq", "tp"),
        P("seq", "tp"),
        P("seq", "tp"),
        P("tp"),
        P("tp"),
        P("tp"),
    )
    out_specs = P("seq", "tp")
    return jax.shard_map(local, mesh=mesh, in_specs=in_specs, out_specs=out_specs, check_vma=False)
```

profile of v0, /device:TPU:49, one launch (start us, length us, event | category | flops | bytes accessed | tf_op | source)
XLA Modules:
  0.0 464.6 jit_solution(14731189784195328036)
XLA Ops:
  6.5 0.0 all-gather.5.cloned.1.call-start
  6.5 0.7 all-gather.5.cloned.1.call-update
  7.3 0.0 all-gather.9.cloned.1.call-start
  7.3 0.7 all-gather.9.cloned.1.call-update
  8.0 0.0 all-gather.11.cloned.1.call-start
  8.1 0.7 all-gather.11.cloned.1.call-update
  8.7 0.7 add_select_fusion
  9.4 1.2 reduce-window.15
  10.6 0.2 slice_reduce_fusion
  10.9 0.1 fusion.32
  11.0 0.2 select_reduce_fusion.1
  11.2 0.1 reduce_sum.55
  11.3 4.3 gather_fusion
  15.7 0.1 gather.17
  15.8 0.2 fusion.11
  16.0 0.1 reduce_or.12
  16.1 0.6 select_select_fusion.1
  16.7 8.3 %all-to-all-start = ((s32[32,1,20]{2,1,0:T(1,128)}), s32[32,1,20]{2,1,0:T(1,128)S(1)}, u32[]{:S(2)}, u32[]{:S(2)}) async-start(s32[32,1,20]{2,1,0:T(1,128)} %bitcast.2), calls=%async_computation | async-start | bytes 32768 | tf_op jit(solution)/shard_map/all_to_all | solution.py:71
  25.0 0.1 reduce_sum.58
  25.1 0.1 broadcast_in_dim.112
  25.2 68.5 %all-gather.5.cloned.1.call-done = bf16[512,8192]{1,0:T(8,128)(2,1)} async-done(((bf16[512,2048]{1,0:T(8,128)(2,1)}), bf16[512,8192]{1,0:T(8,128)(2,1)}) %all-gather.5.cloned.1.call-update) | async-done | bytes 8388624 | tf_op jit(solution)/shard_map/all_gather | solution.py:61
  93.7 25.9 %gather_fusion.1 = bf16[640,8192]{1,0:T(8,128)(2,1)} fusion(bf16[512,8192]{1,0:T(8,128)(2,1)} %all-gather.5.cloned.1.call-done, s32[1024]{0:T(1024)S(1)} %pad_clamp_fusion.1), kind=kCustom, calls=%fused_computation.1 | custom fusion | bytes 20974080 | tf_op jit(solution)/shard_map/jit(_take)/gather | solution.py:62
  119.6 14.2 %gather.19 = bf16[32,20,8192]{2,1,0:T(8,128)(2,1)} reshape(bf16[640,8192]{1,0:T(8,128)(2,1)} %gather_fusion.1) | data formatting | bytes 20971520 | tf_op jit(solution)/shard_map/jit(_take)/gather | solution.py:62
  133.8 10.8 %select_select_fusion = bf16[32,20,8192]{2,1,0:T(8,128)(2,1)} fusion(bf16[32,20,8192]{2,1,0:T(8,128)(2,1)} %gather.19, pred[32,20]{1,0:T(8,128)(4,1)S(1)} %compare_and_fusion, pred[32,20]{1,0:T(8,128)(4,1)S(1)} %broadcast_in_dim.112), kind=kLoop, calls=%fused_computation.8 | loop fusion | flops 10485760 | bytes 20972800 | tf_op jit(solution)/shard_map/jit(_where)/select_n | solution.py:63
  144.7 0.0 all-to-all-done
  144.7 8.0 %all-to-all-start.1 = ((bf16[32,20,8192]{2,1,0:T(8,128)(2,1)}), bf16[32,20,8192]{2,1,0:T(8,128)(2,1)}, u32[]{:S(2)}, u32[]{:S(2)}) async-start(bf16[32,20,8192]{2,1,0:T(8,128)(2,1)} %select_select_fusion), calls=%async_computation.1 | async-start | bytes 25165824 | tf_op jit(solution)/shard_map/all_to_all | solution.py:64
  152.7 0.5 all-gather.7.cloned.1.call-start
  153.2 0.1 all-gather.7.cloned.1.call-update
  153.3 0.0 copy-done.1
  153.3 0.1 slice_compare_fusion
  153.3 0.1 add_select_fusion.2
  153.4 0.3 reduce-window.19
  153.7 0.1 slice.36
  153.8 0.1 slice_reduce_fusion.1
  154.0 0.1 fusion.37
  154.0 0.2 fusion.19
  154.3 1.0 multiply_cosine_fusion
  155.2 0.5 broadcast.313
  155.8 0.7 reduce.11
  156.4 0.1 eq.80
  156.6 0.2 select_reduce_fusion
  156.8 214.4 %all-to-all-done.1 = bf16[32,20,8192]{2,1,0:T(8,128)(2,1)} async-done(((bf16[32,20,8192]{2,1,0:T(8,128)(2,1)}), bf16[32,20,8192]{2,1,0:T(8,128)(2,1)}, u32[]{:S(2)}, u32[]{:S(2)}) %all-to-all-start.1) | async-done | bytes 10485792 | tf_op jit(solution)/shard_map/all_to_all | solution.py:64
  371.2 14.6 %reshape.370 = bf16[640,8192]{1,0:T(8,128)(2,1)} reshape(bf16[32,20,8192]{2,1,0:T(8,128)(2,1)} %all-to-all-done.1) | data formatting | bytes 20971520 | tf_op jit(solution)/shard_map/reshape | solution.py:72
  385.7 20.8 %gather_fusion.2 = bf16[512,8192]{1,0:T(8,128)(2,1)} fusion(bf16[640,8192]{1,0:T(8,128)(2,1)} %reshape.370, s32[1024]{0:T(1024)S(1)} %pad_clamp_fusion), kind=kCustom, calls=%fused_computation.2 | custom fusion | bytes 16779264 | tf_op jit(solution)/shard_map/jit(_take)/gather | solution.py:75
  406.6 5.7 %fusion = f32[512]{0:T(512)S(1)} fusion(bf16[512,8192]{1,0:T(8,128)(2,1)} %gather_fusion.2, pred[512]{0:T(512)(128)(4,1)S(1)} %compare_and_fusion.1), kind=kLoop, calls=%fused_computation.5 | loop fusion | flops 16776704 | bytes 8391168 | tf_op jit(solution)/shard_map/reduce_sum | solution.py:77
  412.3 0.0 copy-start.3
  412.3 0.0 all-gather.9.cloned.1.call-done
  412.3 0.0 copy-done.2
  412.4 0.0 copy-done.4
  412.4 7.3 %fusion.12 = f32[512,1,128]{0,2,1:T(8,128)S(1)} fusion(bf16[8192,128]{1,0:T(8,128)(2,1)} %all-gather.9.cloned.1.call-done, f32[128]{0:T(128)S(1)} %copy-done.4, f32[8192]{0:T(1024)S(1)} %copy-done.2, f32[512]{0:T(512)S(1)} %add_rsqrt_fusion, bf16[512,8192]{1,0:T(8,128)(2,1)} %gather_fusion.2, pred[512]{0:T(512)(128)(4,1)S(1)} %compare_and_fusion.1), kind=kOutput, calls=%fused_computation.28 | convolution fusion | flops 1094778880 | bytes 10783744 | tf_op jit(solution)/shard_map/dot_general | solution.py:81
  419.6 0.6 fusion.34
  420.2 0.0 all-gather.11.cloned.1.call-done
  420.2 0.0 copy-done.3
  420.3 15.2 %add_bitcast_fusion = f32[64,8,8,128]{3,1,2,0:T(8,128)S(1)} fusion(bf16[8192,1024]{1,0:T(8,128)(2,1)} %all-gather.11.cloned.1.call-done, f32[1024]{0:T(1024)S(1)} %copy-done.3, f32[8192]{0:T(1024)S(1)} %copy-done.2, f32[512]{0:T(512)S(1)} %add_rsqrt_fusion, bf16[512,8192]{1,0:T(8,128)(2,1)} %gather_fusion.2, pred[512]{0:T(512)(128)(4,1)S(1)} %compare_and_fusion.1), kind=kOutput, calls=%fused_computation.20 | convolution fusion | flops 8611430400 | bytes 27302400 | tf_op jit(solution)/shard_map/dot_general | solution.py:81
  435.4 0.5 copy.46
  435.9 0.7 fusion.46
  436.6 0.8 subtract_convert_fusion
  437.4 0.0 copy-start.5
  437.4 2.2 fusion.4
  439.6 3.2 copy-done
  442.9 1.7 fusion.3
  444.6 0.0 all-gather.7.cloned.1.call-done
  444.6 11.9 %fusion.8 = bf16[128,8,512]{2,0,1:T(8,128)(2,1)S(1)} fusion(f32[8,512]{1,0:T(8,128)S(1)} %fusion.3, f32[8,512]{1,0:T(8,128)S(1)} %get-tuple-element.15, f32[512,512,8]{1,0,2:T(8,128)} %copy-done, pred[512,512]{0,1:T(8,128)(4,1)S(1)} %fusion.19, bf16[8192,128]{1,0:T(8,128)(2,1)} %all-gather.7.cloned.1.call-done, f32[128]{0:T(128)S(1)} %copy-done.5, ...), kind=kOutput, calls=%fused_computation.21 | convolution fusion | flops 1642725376 | bytes 20253696 | tf_op jit(solution)/shard_map/kgqp,pkd->qkgd/dot_general | solution.py:110
  456.5 1.3 copy.37
  (18 shorter events, 0.2 us)
Async XLA Ops:
  6.5 87.2 %all-gather.5.cloned.1.call-start = ((), (), s32[]{:S(2)}) async-start(), calls=%async_computation.2 | async-start | bytes 10485760 | tf_op jit(solution)/shard_map/all_gather | solution.py:61
  7.3 405.1 %all-gather.9.cloned.1.call-start = ((), (), s32[]{:S(2)}) async-start(), calls=%async_computation.4 | async-start | bytes 2162688 | tf_op jit(solution)/shard_map/all_gather | solution.py:84
  8.0 412.2 %all-gather.11.cloned.1.call-start = ((), (), s32[]{:S(2)}) async-start(), calls=%async_computation.5 | async-start | bytes 17301504 | tf_op jit(solution)/shard_map/all_gather | solution.py:83
  16.7 128.0 %all-to-all-start = ((s32[32,1,20]{2,1,0:T(1,128)}), s32[32,1,20]{2,1,0:T(1,128)S(1)}, u32[]{:S(2)}, u32[]{:S(2)}) async-start(s32[32,1,20]{2,1,0:T(1,128)} %bitcast.2), calls=%async_computation | async-start | bytes 32768 | tf_op jit(solution)/shard_map/all_to_all | solution.py:71
  144.7 8.6 %copy-start.1 = (s32[512]{0:T(512)S(1)}, s32[512]{0:T(512)}, u32[]{:S(2)}) copy-start(s32[512]{0:T(512)} %param.12) | copy-start | bytes 6148
  144.7 226.5 %all-to-all-start.1 = ((bf16[32,20,8192]{2,1,0:T(8,128)(2,1)}), bf16[32,20,8192]{2,1,0:T(8,128)(2,1)}, u32[]{:S(2)}, u32[]{:S(2)}) async-start(bf16[32,20,8192]{2,1,0:T(8,128)(2,1)} %select_select_fusion), calls=%async_computation.1 | async-start | bytes 25165824 | tf_op jit(solution)/shard_map/all_to_all | solution.py:64
  152.7 291.9 %all-gather.7.cloned.1.call-start = ((), (), s32[]{:S(2)}) async-start(), calls=%async_computation.3 | async-start | bytes 2162688 | tf_op jit(solution)/shard_map/all_gather | solution.py:85
  406.6 5.8 %copy-start.2 = (f32[8192]{0:T(1024)S(1)}, f32[8192]{0:T(1024)}, u32[]{:S(2)}) copy-start(f32[8192]{0:T(1024)} %param.13) | copy-start | bytes 98308
  406.6 5.8 %copy-start.4 = (f32[128]{0:T(128)S(1)}, f32[128]{0:T(128)}, u32[]{:S(2)}) copy-start(f32[128]{0:T(128)} %param.18) | copy-start | bytes 1540
  412.3 7.9 %copy-start.3 = (f32[1024]{0:T(1024)S(1)}, f32[1024]{0:T(1024)}, u32[]{:S(2)}) copy-start(f32[1024]{0:T(1024)} %param.17) | copy-start | bytes 12292
  437.4 7.2 %copy-start.5 = (f32[128]{0:T(128)S(1)}, f32[128]{0:T(128)}, u32[]{:S(2)}) copy-start(f32[128]{0:T(128)} %param.19) | copy-start | bytes 1540
  439.6 3.2 copy-start
Sparse Core Ops, SparseCore 0:
  9.0 84.6 all-gather.4
  96.0 43.3 all-gather.8
  141.7 200.8 all-gather.10
  344.7 44.3 all-gather.6
where the time goes:
time: 474 us; the launch traced here: 465 us
  waiting for transfers between devices  285 us (60%)
  local copies, waits for them, and re-layouts  87 us (18%)
  matrix products  36.6 us (8%)
  other arithmetic  25.5 us (5%)
  starting transfers between devices  16.8 us (4%)
  between operations  13.6 us (3%)
    all_to_all x1, waiting for transfers between devices, local(): lax.all_to_all(picked.reshape(peer_count, slots_each, full_rows.shape[1])...  214 us
    all_gather x1, waiting for transfers between devices, local(): full_rows = lax.all_gather(rollout_rows, 'tp', axis=1, tiled=True)  68.5 us
    gather x2, local copies, waits for them, and re-layouts, local(): picked = jnp.take(full_rows, source_index, axis=0)  40.1 us
    dot_general x2, matrix products, add_rows(): return jnp.dot(normed, weight_piece, preferred_element_type=jnp.float32)  22.4 us
    gather x1, local copies, waits for them, and re-layouts, local(): learner_rows = jnp.take(flat_rows, slot_of_row, axis=0)  20.8 us
    reshape x1, local copies, waits for them, and re-layouts, local(): flat_rows = arrived.reshape(slot_total, arrived.shape[2])  14.6 us
    dot_general x1, matrix products, local(): jnp.einsum('kgqp,pkd->qkgd', probs, value_heads, preferred_element_type=j...  11.9 us
    select_n x1, other arithmetic, local(): picked = jnp.where(filled[:, None], picked, jnp.zeros_like(picked))  10.8 us
  transfers between devices with their start and end apart: 6, of which 2 were waited for; matrix products, arithmetic and copies ran while one was open for 29% of the time, Pallas kernels for 0%

commit v1 on v0

v1 whole, which is shorter than its diff:
```python
import math

import jax
import jax.numpy as jnp
from jax import lax
from jax.sharding import Mesh
from jax.sharding import PartitionSpec as P


HEAD = 128


EPS = 1e-06
ROPE_BASE = 1000000.0

CHIPS = "chips"
CORE = "core"
SEQ = (CHIPS, CORE)
TP = "tp"


def rotate(tensor, positions):
    half_size = tensor.shape[-1] // 2
    frequency = jnp.exp(
        jnp.arange(half_size, dtype=jnp.float32) * (-2.0 * math.log(ROPE_BASE) / tensor.shape[-1])
    )
    angles = positions.astype(jnp.float32)[:, None] * frequency[None, :]
    cosine = jnp.cos(angles)[:, None, :]
    sine_part = jnp.sin(angles)[:, None, :]
    front_half = tensor[..., :half_size]
    back_half = tensor[..., half_size:]
    return jnp.concatenate(
        [front_half * cosine - back_half * sine_part, back_half * cosine + front_half * sine_part],
        axis=-1,
    )


def positions_of(segments):
    length = segments.shape[-1]
    counter = jnp.arange(length, dtype=jnp.int32)
    starts = jnp.concatenate([jnp.ones((1,), dtype=bool), segments[1:] != segments[:-1]])
    marked = jnp.where(starts, counter, jnp.zeros_like(counter))
    return counter - lax.cummax(marked, axis=0)


def make_local(chip_count, core_count, tp_count):
    peer_count = chip_count * core_count

    def body(
        rollout_rows, plan, segment_ids, norm_gain, q_weight, k_weight, v_weight, q_bias, k_bias, v_bias
    ):
        row_count, width = rollout_rows.shape
        slots_each = row_count // peer_count + row_count // (4 * peer_count)
        slot_total = peer_count * slots_each
        q_cols = q_weight.shape[1]
        k_cols = k_weight.shape[1]
        depth = q_weight.shape[0]

        weights = jnp.concatenate([q_weight, k_weight, v_weight], axis=1)
        chip_weights = lax.all_gather(weights, CHIPS, axis=0, tiled=False)
        full_weights = lax.all_gather(chip_weights, CORE, axis=0, tiled=False)

        target = plan // row_count
        learner_slot = plan % row_count
        matches = (target[:, None] == jnp.arange(peer_count, dtype=jnp.int32)[None, :]).astype(
            jnp.int32
        )
        ranking = jnp.sum((jnp.cumsum(matches, axis=0) - 1) * matches, axis=1)
        flat_slot = target * slots_each + ranking
        slot_numbers = jnp.arange(slot_total, dtype=jnp.int32)
        row_numbers = jnp.arange(row_count, dtype=jnp.int32)
        slot_hits = flat_slot[None, :] == slot_numbers[:, None]
        parcels = (
            jnp.sum(jnp.where(slot_hits, learner_slot[None, :] + 1, 0), axis=1) - 1
        ).reshape(peer_count, slots_each)
        labels = lax.all_to_all(parcels, SEQ, split_axis=0, concat_axis=0, tiled=True)
        picked = jnp.dot(
            slot_hits.astype(jnp.bfloat16), rollout_rows, preferred_element_type=jnp.float32
        ).astype(jnp.bfloat16)
        arrived = lax.all_to_all(
            picked.reshape(peer_count, slots_each, width),
            SEQ,
            split_axis=0,
            concat_axis=0,
            tiled=True,
        )
        label_hits = labels.reshape(slot_total)[None, :] == row_numbers[:, None]
        learner_part = jnp.dot(
            label_hits.astype(jnp.bfloat16),
            arrived.reshape(slot_total, width),
            preferred_element_type=jnp.float32,
        ).astype(jnp.bfloat16)
        spread = jnp.broadcast_to(learner_part[None], (tp_count, row_count, width))
        quarters = lax.all_to_all(spread, TP, split_axis=0, concat_axis=0, tiled=True)
        widened = quarters.astype(jnp.float32)
        mean_sq = jnp.sum(widened * widened, axis=(0, 2), keepdims=True) / (width * tp_count)
        gain = norm_gain.reshape(tp_count, 1, width)
        normed = (widened * lax.rsqrt(mean_sq + EPS) * gain).astype(jnp.bfloat16)
        normed = normed.transpose(1, 0, 2).reshape(row_count, chip_count, core_count, depth)
        projected = jnp.einsum(
            "rhcj,chjn->rn", normed, full_weights, preferred_element_type=jnp.float32
        )
        queries = projected[:, :q_cols]
        key_proj = projected[:, q_cols : q_cols + k_cols]
        value_proj = projected[:, q_cols + k_cols :]
        local_heads = q_cols // HEAD
        local_groups = k_cols // HEAD
        group_size = local_heads // local_groups
        positions = positions_of(segment_ids)
        q_rot = rotate((queries + q_bias).reshape(row_count, local_heads, HEAD), positions).astype(
            jnp.bfloat16
        )
        q_rot = q_rot.reshape(row_count, local_groups, group_size, HEAD)
        k_rot = rotate((key_proj + k_bias).reshape(row_count, local_groups, HEAD), positions).astype(
            jnp.bfloat16
        )
        value_heads = (value_proj + v_bias).astype(jnp.bfloat16).reshape(row_count, local_groups, HEAD)
        block_rows = min(512, row_count)
        row_index = jnp.arange(row_count, dtype=jnp.int32)
        scores = jnp.einsum(
            "qkgd,pkd->kgqp", q_rot, k_rot, preferred_element_type=jnp.float32
        ) / math.sqrt(HEAD)
        allowed = (segment_ids[0:block_rows, None] == segment_ids[None, :block_rows]) & (
            row_index[0:block_rows, None] >= row_index[None, :block_rows]
        )
        scores = jnp.where(allowed[None, None], scores, -jnp.inf)
        highest = jnp.max(scores, axis=-1, keepdims=True)
        expo = jnp.exp(scores - highest)
        probs = (expo / jnp.sum(expo, axis=-1, keepdims=True)).astype(jnp.bfloat16)
        mixed = jnp.einsum("kgqp,pkd->qkgd", probs, value_heads, preferred_element_type=jnp.float32)
        outputs = mixed.astype(jnp.bfloat16).reshape(block_rows, local_heads * HEAD)
        return outputs

    return body


def solution(mesh):
    seq_count, tp_count = mesh.devices.shape
    core_count = 2
    chip_count = seq_count // core_count
    split = Mesh(mesh.devices.reshape(chip_count, core_count, tp_count), (CHIPS, CORE, TP))
    in_specs = (
        P(SEQ, TP),
        P(SEQ),
        P(SEQ),
        P(),
        P(SEQ, TP),
        P(SEQ, TP),
        P(SEQ, TP),
        P(TP),
        P(TP),
        P(TP),
    )
    out_specs = P(SEQ, TP)
    return jax.shard_map(
        make_local(chip_count, core_count, tp_count),
        mesh=split,
        in_specs=in_specs,
        out_specs=out_specs,
        check_vma=False,
    )
```

time: 474 us -> 324 us (0.68)
  waiting for transfers between devices: 285 us -> 209 us
  local copies, waits for them, and re-layouts: 87 us -> 22.5 us
  matrix products: 36.6 us -> 29.8 us
    all_to_all x2 -> x3, waiting for transfers between devices: 214 us -> 127 us  [the longest x1 91.9 us: body(): lax.all_to_all(spread, TP, split_axis=0, concat_axis=0, tiled=True)]
    gather x5 -> x0, local copies, waits for them, and re-layouts: 65.3 us -> none  [the longest x2 40.1 us: local(): picked = jnp.take(full_rows, source_index, axis=0)]
    all_gather x4 -> x2, waiting for transfers between devices: 68.6 us -> 81.5 us  [the longest x1 81.5 us: body(): chip_weights = lax.all_gather(weights, CHIPS, axis=0, tiled=False)]
    select_n x5 -> x0, other arithmetic: 12.2 us -> none  [the longest x1 10.8 us: local(): picked = jnp.where(filled[:, None], picked, jnp.zeros_like(picked))]
    convert_element_type x1 -> x2, other arithmetic: 0.01 us -> 7.85 us  [the longest x1 7.84 us: body(): normed = (widened * lax.rsqrt(mean_sq + EPS) * gain).astype(jnp.bfloat16)]
    dot_general x4 -> x5, matrix products: 36.6 us -> 29.8 us  [the longest x1 17 us: body(): jnp.einsum('rhcj,chjn->rn', normed, full_weights, preferred_element_type=...]
    all_to_all x2 -> x3, starting transfers between devices: 16.2 us -> 20.9 us  [the longest x1 7.62 us: body(): lax.all_to_all(parcels, SEQ, split_axis=0, concat_axis=0, tiled=True)]
    reshape x2 -> x3, local copies, waits for them, and re-layouts: 15.9 us -> 12.1 us  [the longest x1 5.64 us: body(): picked.reshape(peer_count, slots_each, width)]
  transfers between devices with their start and end apart: 6 -> 5, of which waited for: 2 -> 3; matrix products, arithmetic and copies ran while one was open for 29% -> 14% of each run, Pallas kernels for 0% -> 0%
where the time goes in v1:
time: 324 us; the launch traced here: 319 us
  waiting for transfers between devices  209 us (65%)
  matrix products  29.8 us (9%)
  other arithmetic  23.4 us (7%)
  local copies, waits for them, and re-layouts  22.5 us (7%)
  starting transfers between devices  20.9 us (6%)
  between operations  13.6 us (4%)
    all_to_all x1, waiting for transfers between devices, body(): lax.all_to_all(spread, TP, split_axis=0, concat_axis=0, tiled=True)  91.9 us
    all_gather x1, waiting for transfers between devices, body(): chip_weights = lax.all_gather(weights, CHIPS, axis=0, tiled=False)  81.5 us
    all_to_all x1, waiting for transfers between devices, body(): lax.all_to_all(picked.reshape(peer_count, slots_each, width), SEQ, split_...  35.3 us
    dot_general x1, matrix products, body(): jnp.einsum('rhcj,chjn->rn', normed, full_weights, preferred_element_type=...  17 us
    convert_element_type x1, other arithmetic, body(): normed = (widened * lax.rsqrt(mean_sq + EPS) * gain).astype(jnp.bfloat16)  7.84 us
    all_to_all x1, starting transfers between devices, body(): lax.all_to_all(parcels, SEQ, split_axis=0, concat_axis=0, tiled=True)  7.62 us
    all_to_all x1, starting transfers between devices, body(): lax.all_to_all(picked.reshape(peer_count, slots_each, width), SEQ, split_...  7.36 us
  transfers between devices with their start and end apart: 5, of which 3 were waited for; matrix products, arithmetic and copies ran while one was open for 14% of the time, Pallas kernels for 0%

profile of v1, /device:TPU:49, one launch (start us, length us, event | category | flops | bytes accessed | tf_op | source)
XLA Modules:
  0.0 319.1 jit_solution(14747195369925813049)
XLA Ops:
  6.5 0.0 copy-start
  6.5 0.0 all-gather.5.cloned.1.call-start
  6.5 2.1 pad_maximum_fusion
  8.7 0.0 all-gather.5.cloned.1.call-update
  8.7 0.0 all-gather.7.cloned.1.call-start
  8.8 81.5 %all-gather.5.cloned.1.call-done = bf16[4096,1280]{1,0:T(8,128)(2,1)} async-done(((bf16[256,1280]{1,0:T(8,128)(2,1)}), bf16[4096,1280]{1,0:T(8,128)(2,1)}) %all-gather.5.cloned.1.call-update) | async-done | bytes 10485776 | tf_op jit(solution)/shard_map/all_gather | solution.py:60
  90.3 0.0 copy-start.5
  90.3 0.0 all-gather.7.cloned.1.call-update
  90.3 0.7 copy-done.5
  91.0 1.2 reduce-window.15
  92.1 0.2 slice_reduce_fusion
  92.4 0.1 fusion.42
  92.5 0.2 select_reduce_fusion
  92.8 0.7 sub.46
  93.5 7.6 %all-to-all-start = ((s32[32,1,20]{2,1,0:T(1,128)}), s32[32,1,20]{2,1,0:T(1,128)S(1)}, u32[]{:S(2)}, u32[]{:S(2)}) async-start(s32[32,1,20]{2,1,0:T(1,128)} %bitcast.2), calls=%async_computation | async-start | bytes 32768 | tf_op jit(solution)/shard_map/all_to_all | solution.py:76
  101.1 0.0 copy-done
  101.1 3.1 convolution_convert_fusion
  104.2 5.6 %reshape.284 = bf16[32,20,2048]{2,1,0:T(8,128)(2,1)} reshape(bf16[640,2048]{1,0:T(8,128)(2,1)} %convolution_convert_fusion) | data formatting | bytes 5242880 | tf_op jit(solution)/shard_map/reshape | solution.py:81
  109.8 0.0 all-to-all-done
  109.8 7.4 %all-to-all-start.1 = ((bf16[32,20,2048]{2,1,0:T(8,128)(2,1)}), bf16[32,20,2048]{2,1,0:T(8,128)(2,1)}, u32[]{:S(2)}, u32[]{:S(2)}) async-start(bf16[32,20,2048]{2,1,0:T(8,128)(2,1)} %reshape.284), calls=%async_computation.1 | async-start | bytes 6291456 | tf_op jit(solution)/shard_map/all_to_all | solution.py:80
  117.2 0.5 broadcast.212
  117.7 0.7 reduce.9
  118.4 0.1 eq.80
  118.5 35.3 %all-to-all-done.1 = bf16[32,20,2048]{2,1,0:T(8,128)(2,1)} async-done(((bf16[32,20,2048]{2,1,0:T(8,128)(2,1)}), bf16[32,20,2048]{2,1,0:T(8,128)(2,1)}, u32[]{:S(2)}, u32[]{:S(2)}) %all-to-all-start.1) | async-done | bytes 2621472 | tf_op jit(solution)/shard_map/all_to_all | solution.py:80
  153.8 5.2 %reshape.285 = bf16[640,2048]{1,0:T(8,128)(2,1)} reshape(bf16[32,20,2048]{2,1,0:T(8,128)(2,1)} %all-to-all-done.1) | data formatting | bytes 5242880 | tf_op jit(solution)/shard_map/reshape | solution.py:90
  159.0 4.9 %convolution_convert_fusion.1 = bf16[512,2048]{1,0:T(8,128)(2,1)} fusion(bf16[640,2048]{1,0:T(8,128)(2,1)} %reshape.285, s32[640]{0:T(1024)S(1)} %eq.80), kind=kOutput, calls=%fused_computation.17 | convolution fusion | flops 1343553536 | bytes 4721152 | tf_op jit(solution)/shard_map/dot_general | solution.py:88
  163.8 2.9 copy.35
  166.7 3.9 %broadcast_in_dim.24 = bf16[4,512,2048]{1,2,0:T(8,128)(2,1)} broadcast(bf16[512,2048]{0,1:T(8,128)(2,1)S(1)} %copy.35), dimensions={1,2} | broadcast | bytes 10485760 | tf_op jit(solution)/shard_map/broadcast_in_dim | solution.py:93
  170.6 0.0 copy-start.3
  170.6 0.0 copy-start.2
  170.6 5.9 %all-to-all-start.2 = ((bf16[4,512,2048]{1,2,0:T(8,128)(2,1)}), bf16[4,512,2048]{1,2,0:T(8,128)(2,1)}, u32[]{:S(2)}, u32[]{:S(2)}) async-start(bf16[4,512,2048]{1,2,0:T(8,128)(2,1)} %broadcast_in_dim.24), calls=%async_computation.2 | async-start | bytes 16777216 | tf_op jit(solution)/shard_map/all_to_all | solution.py:94
  176.5 0.0 copy-done.3
  176.6 0.0 copy-done.2
  176.6 0.1 slice_compare_fusion
  176.7 0.1 add_select_fusion.2
  176.7 0.3 reduce-window.19
  177.0 0.1 slice.47
  177.2 0.1 slice_reduce_fusion.1
  177.3 0.1 fusion.45
  177.4 0.2 fusion.21
  177.6 1.0 multiply_cosine_fusion
  178.6 91.9 %all-to-all-done.2 = bf16[4,512,2048]{1,2,0:T(8,128)(2,1)} async-done(((bf16[4,512,2048]{1,2,0:T(8,128)(2,1)}), bf16[4,512,2048]{1,2,0:T(8,128)(2,1)}, u32[]{:S(2)}, u32[]{:S(2)}) %all-to-all-start.2) | async-done | bytes 8388640 | tf_op jit(solution)/shard_map/all_to_all | solution.py:94
  270.4 5.2 %fusion = f32[512]{0:T(512)S(1)} fusion(bf16[4,512,2048]{1,2,0:T(8,128)(2,1)} %all-to-all-done.2), kind=kLoop, calls=%fused_computation.2 | loop fusion | flops 12582400 | bytes 8390656 | tf_op jit(solution)/shard_map/reduce_sum | solution.py:96
  275.6 7.8 %fusion.2 = bf16[4,512,2048]{1,2,0:T(8,128)(2,1)} fusion(bf16[4,512,2048]{1,2,0:T(8,128)(2,1)} %all-to-all-done.2, f32[4,2048]{1,0:T(4,128)S(1)} %mul.125, f32[512]{0:T(512)S(1)} %add_rsqrt_fusion), kind=kLoop, calls=%fused_computation.4 | loop fusion | flops 16777216 | bytes 16812032 | tf_op jit(solution)/shard_map/convert_element_type | solution.py:98
  283.5 0.0 all-gather.7.cloned.1.call-done
  283.5 0.0 copy-start.4
  283.5 17.0 %fusion.10 = f32[512,1280]{1,0:T(8,128)S(1)} fusion(bf16[2,16,256,1280]{3,2,1,0:T(8,128)(2,1)} %bitcast.84, bf16[512,16,2,256]{0,3,2,1:T(8,128)(2,1)} %bitcast.81), kind=kOutput, calls=%fused_computation.15 | convolution fusion | flops 10737418240 | bytes 31981568 | tf_op jit(solution)/shard_map/rhcj,chjn->rn/dot_general | solution.py:100
  300.5 0.0 copy-done.4
  300.5 0.3 fusion.13
  300.8 0.5 copy.51
  301.2 0.0 copy-start.6
  301.3 0.7 fusion.50
  301.9 0.0 copy-done.6
  302.0 1.4 fusion.40
  303.4 0.8 subtract_convert_fusion
  304.2 2.2 fusion.6
  306.4 0.0 copy-start.7
  306.5 1.7 fusion.5
  308.2 0.0 copy-done.7
  308.2 0.0 copy-start.1
  308.2 2.7 fusion.14
  310.9 1.3 copy.41
  312.2 0.0 copy-done.1
  (11 shorter events, 0.2 us)
Async XLA Ops:
  6.5 94.6 %copy-start = (bf16[512,2048]{1,0:T(8,128)(2,1)S(1)}, bf16[512,2048]{1,0:T(8,128)(2,1)}, u32[]{:S(2)}) copy-start(bf16[512,2048]{1,0:T(8,128)(2,1)} %param.10) | copy-start | bytes 6291460
  6.5 83.7 %all-gather.5.cloned.1.call-start = ((), (), s32[]{:S(2)}) async-start(), calls=%async_computation.3 | async-start | bytes 11141120 | tf_op jit(solution)/shard_map/all_gather | solution.py:60
  8.7 274.8 %all-gather.7.cloned.1.call-start = ((), (), s32[]{:S(2)}) async-start(), calls=%async_computation.4 | async-start | bytes 31457280 | tf_op jit(solution)/shard_map/all_gather | solution.py:61
  90.3 0.7 copy-start.5
  93.5 16.4 %all-to-all-start = ((s32[32,1,20]{2,1,0:T(1,128)}), s32[32,1,20]{2,1,0:T(1,128)S(1)}, u32[]{:S(2)}, u32[]{:S(2)}) async-start(s32[32,1,20]{2,1,0:T(1,128)} %bitcast.2), calls=%async_computation | async-start | bytes 32768 | tf_op jit(solution)/shard_map/all_to_all | solution.py:76
  109.8 44.0 %all-to-all-start.1 = ((bf16[32,20,2048]{2,1,0:T(8,128)(2,1)}), bf16[32,20,2048]{2,1,0:T(8,128)(2,1)}, u32[]{:S(2)}, u32[]{:S(2)}) async-start(bf16[32,20,2048]{2,1,0:T(8,128)(2,1)} %reshape.284), calls=%async_computation.1 | async-start | bytes 6291456 | tf_op jit(solution)/shard_map/all_to_all | solution.py:80
  170.6 5.9 %copy-start.3 = (f32[8192]{0:T(1024)S(1)}, f32[8192]{0:T(1024)}, u32[]{:S(2)}) copy-start(f32[8192]{0:T(1024)} %param.13) | copy-start | bytes 98308
  170.6 6.0 %copy-start.2 = (s32[512]{0:T(512)S(1)}, s32[512]{0:T(512)}, u32[]{:S(2)}) copy-start(s32[512]{0:T(512)} %param.12) | copy-start | bytes 6148
  170.6 99.8 %all-to-all-start.2 = ((bf16[4,512,2048]{1,2,0:T(8,128)(2,1)}), bf16[4,512,2048]{1,2,0:T(8,128)(2,1)}, u32[]{:S(2)}, u32[]{:S(2)}) async-start(bf16[4,512,2048]{1,2,0:T(8,128)(2,1)} %broadcast_in_dim.24), calls=%async_computation.2 | async-start | bytes 16777216 | tf_op jit(solution)/shard_map/all_to_all | solution.py:94
  283.5 17.0 %copy-start.4 = (f32[1024]{0:T(1024)S(1)}, f32[1024]{0:T(1024)}, u32[]{:S(2)}) copy-start(f32[1024]{0:T(1024)} %param.17) | copy-start | bytes 12292
  301.2 0.7 copy-start.6
  306.4 1.8 copy-start.7
  308.2 4.0 %copy-start.1 = (bf16[512,2048]{1,0:T(8,128)(2,1)S(1)}, bf16[512,2048]{1,0:T(8,128)(2,1)}, u32[]{:S(2)}) copy-start(bf16[512,2048]{1,0:T(8,128)(2,1)} %param.10) | copy-start | bytes 6291460
Sparse Core Ops, SparseCore 0:
  9.5 80.6 all-gather.4
  91.9 40.1 all-gather.6

commit v2 on v1

--- a/solution.py
+++ b/solution.py
@@ -51,14 +51,15 @@
     ):
         row_count, width = rollout_rows.shape
         slots_each = row_count // peer_count + row_count // (4 * peer_count)
-        slot_total = peer_count * slots_each
         q_cols = q_weight.shape[1]
         k_cols = k_weight.shape[1]
         depth = q_weight.shape[0]
 
         weights = jnp.concatenate([q_weight, k_weight, v_weight], axis=1)
-        chip_weights = lax.all_gather(weights, CHIPS, axis=0, tiled=False)
-        full_weights = lax.all_gather(chip_weights, CORE, axis=0, tiled=False)
+        own_weights = lax.all_gather(weights, CHIPS, axis=0, tiled=False)
+        other_weights = lax.ppermute(
+            own_weights, CORE, [(c, (c + 1) % core_count) for c in range(core_count)]
+        )
 
         target = plan // row_count
         learner_slot = plan % row_count
@@ -66,40 +67,51 @@
             jnp.int32
         )
         ranking = jnp.sum((jnp.cumsum(matches, axis=0) - 1) * matches, axis=1)
-        flat_slot = target * slots_each + ranking
-        slot_numbers = jnp.arange(slot_total, dtype=jnp.int32)
-        row_numbers = jnp.arange(row_count, dtype=jnp.int32)
-        slot_hits = flat_slot[None, :] == slot_numbers[:, None]
-        parcels = (
-            jnp.sum(jnp.where(slot_hits, learner_slot[None, :] + 1, 0), axis=1) - 1
-        ).reshape(peer_count, slots_each)
+        slot_hits = (target[None, None, :] == jnp.arange(peer_count, dtype=jnp.int32)[:, None, None]) & (
+            ranking[None, None, :] == jnp.arange(slots_each, dtype=jnp.int32)[None, :, None]
+        )
+        parcels = jnp.sum(jnp.where(slot_hits, learner_slot[None, None, :] + 1, 0), axis=2) - 1
         labels = lax.all_to_all(parcels, SEQ, split_axis=0, concat_axis=0, tiled=True)
-        picked = jnp.dot(
-            slot_hits.astype(jnp.bfloat16), rollout_rows, preferred_element_type=jnp.float32
-        ).astype(jnp.bfloat16)
-        arrived = lax.all_to_all(
-            picked.reshape(peer_count, slots_each, width),
-            SEQ,
-            split_axis=0,
-            concat_axis=0,
-            tiled=True,
-        )
-        label_hits = labels.reshape(slot_total)[None, :] == row_numbers[:, None]
-        learner_part = jnp.dot(
-            label_hits.astype(jnp.bfloat16),
-            arrived.reshape(slot_total, width),
+        picked = jnp.einsum(
+            "psr,rf->psf",
+            slot_hits.astype(jnp.bfloat16),
+            rollout_rows,
             preferred_element_type=jnp.float32,
         ).astype(jnp.bfloat16)
-        spread = jnp.broadcast_to(learner_part[None], (tp_count, row_count, width))
-        quarters = lax.all_to_all(spread, TP, split_axis=0, concat_axis=0, tiled=True)
+        arrived = lax.all_to_all(picked, SEQ, split_axis=0, concat_axis=0, tiled=True)
+        row_numbers = jnp.arange(row_count, dtype=jnp.int32)
+        label_hits = labels[None, :, :] == row_numbers[:, None, None]
+        learner_part = jnp.einsum(
+            "rps,psf->rf",
+            label_hits.astype(jnp.bfloat16),
+            arrived,
+            preferred_element_type=jnp.float32,
+        ).astype(jnp.bfloat16)
+
+        to_right = [(t, (t + 1) % tp_count) for t in range(tp_count)]
+        to_left = [(t, (t - 1) % tp_count) for t in range(tp_count)]
+        half = width // 2
+        from_left = lax.ppermute(learner_part, TP, to_right)
+        from_right = lax.ppermute(learner_part, TP, to_left)
+        far_a = lax.ppermute(from_left[:, :half], TP, to_right)
+        far_b = lax.ppermute(from_right[:, half:], TP, to_left)
+        far = jnp.concatenate([far_a, far_b], axis=1)
+        tp_index = lax.axis_index(TP)
+        by_offset = jnp.stack([learner_part, from_left, far, from_right])
+        order = (tp_index - jnp.arange(tp_count, dtype=jnp.int32)) % tp_count
+        inverse = jnp.argsort(order)
+        quarters = jnp.take(by_offset, inverse, axis=0)
         widened = quarters.astype(jnp.float32)
         mean_sq = jnp.sum(widened * widened, axis=(0, 2), keepdims=True) / (width * tp_count)
         gain = norm_gain.reshape(tp_count, 1, width)
         normed = (widened * lax.rsqrt(mean_sq + EPS) * gain).astype(jnp.bfloat16)
         normed = normed.transpose(1, 0, 2).reshape(row_count, chip_count, core_count, depth)
+        core_index = lax.axis_index(CORE)
+        own_cols = jnp.take(normed, core_index, axis=2)
+        other_cols = jnp.take(normed, (core_index + 1) % core_count, axis=2)
         projected = jnp.einsum(
-            "rhcj,chjn->rn", normed, full_weights, preferred_element_type=jnp.float32
-        )
+            "rhj,hjn->rn", own_cols, own_weights, preferred_element_type=jnp.float32
+        ) + jnp.einsum("rhj,hjn->rn", other_cols, other_weights, preferred_element_type=jnp.float32)
         queries = projected[:, :q_cols]
         key_proj = projected[:, q_cols : q_cols + k_cols]
         value_proj = projected[:, q_cols + k_cols :]

time: 324 us -> 308 us (0.951)
  waiting for transfers between devices: 209 us -> 150 us
  local copies, waits for them, and re-layouts: 22.5 us -> 55.6 us
  other arithmetic: 23.4 us -> 29.4 us
    all_to_all x2 -> x1, waiting for transfers between devices: 127 us -> 0.01 us  [body(): lax.all_to_all(picked, SEQ, split_axis=0, concat_axis=0, tiled=True)]
    ppermute x0 -> x5, waiting for transfers between devices: none -> 64.2 us  [the longest x1 45 us: body(): from_left = lax.ppermute(learner_part, TP, to_right)]
    gather x0 -> x3, local copies, waits for them, and re-layouts: none -> 13.6 us  [body(): quarters = jnp.take(by_offset, inverse, axis=0)]
    unnamed x17 -> x31, local copies, waits for them, and re-layouts: 1.16 us -> 13.6 us
    mul x1 -> x2, local copies, waits for them, and re-layouts: 0.02 us -> 11.5 us  [body(): normed = (widened * lax.rsqrt(mean_sq + EPS) * gain).astype(jnp.bfloat16)]
    reshape x2 -> x0, local copies, waits for them, and re-layouts: 10.8 us -> none  [the longest x1 5.64 us: body(): picked.reshape(peer_count, slots_each, width)]
    convert_element_type x1 -> x0, other arithmetic: 7.84 us -> none  [body(): normed = (widened * lax.rsqrt(mean_sq + EPS) * gain).astype(jnp.bfloat16)]
    another operation x3 -> x4, local copies, waits for them, and re-layouts: 0.19 us -> 7.87 us  [the longest x1 7.67 us: body(): other_cols = jnp.take(normed, (core_index + 1) % core_count, axis=2)]
  transfers between devices with their start and end apart: 5 -> 8, of which waited for: 3 -> 4; matrix products, arithmetic and copies ran while one was open for 14% -> 31% of each run, Pallas kernels for 0% -> 0%
where the time goes in v2:
time: 308 us; the launch traced here: 303 us
  waiting for transfers between devices  150 us (49%)
  local copies, waits for them, and re-layouts  55.6 us (18%)
  matrix products  32.3 us (10%)
  other arithmetic  29.4 us (10%)
  starting transfers between devices  21.5 us (7%)
  between operations  13.7 us (4%)
    all_gather x1, waiting for transfers between devices, body(): own_weights = lax.all_gather(weights, CHIPS, axis=0, tiled=False)  86.2 us
    ppermute x1, waiting for transfers between devices, body(): from_left = lax.ppermute(learner_part, TP, to_right)  45 us
    ppermute x1, waiting for transfers between devices, body(): far_a = lax.ppermute(from_left[:, :half], TP, to_right)  17.4 us
    gather x3, local copies, waits for them, and re-layouts, body(): quarters = jnp.take(by_offset, inverse, axis=0)  13.6 us
    unnamed x31, local copies, waits for them, and re-layouts  13.6 us
    mul x2, local copies, waits for them, and re-layouts, body(): normed = (widened * lax.rsqrt(mean_sq + EPS) * gain).astype(jnp.bfloat16)  11.5 us
    dot_general x1, matrix products, body(): jnp.einsum('rhj,hjn->rn', own_cols, own_weights, preferred_element_type=j...  10.7 us
    dot_general x1, matrix products, body(): jnp.einsum('rhj,hjn->rn', other_cols, other_weights, preferred_element_ty...  9.44 us
  transfers between devices with their start and end apart: 8, of which 4 were waited for; matrix products, arithmetic and copies ran while one was open for 31% of the time, Pallas kernels for 0%

profile of v2, /device:TPU:49, one launch (start us, length us, event | category | flops | bytes accessed | tf_op | source)
XLA Modules:
  0.0 302.9 jit_solution(15797872524756142901)
XLA Ops:
  6.5 2.1 pad_maximum_fusion.1
  8.7 0.0 all-gather.3.cloned.1.call-update
  8.7 0.7 fusion.64
  9.4 1.2 reduce-window.15
  10.6 0.2 slice_reduce_fusion
  10.8 0.1 fusion.62
  11.0 0.4 fusion.35
  11.4 0.7 copy.38
  12.1 8.3 %all-to-all-start = ((s32[32,1,20]{2,1,0:T(1,128)}), s32[32,1,20]{2,1,0:T(1,128)S(1)}, u32[]{:S(2)}, u32[]{:S(2)}) async-start(s32[32,1,20]{2,1,0:T(1,128)} %copy.38), calls=%async_computation | async-start | bytes 32768 | tf_op jit(solution)/shard_map/all_to_all | solution.py:74
  20.4 1.5 convolution_convert_fusion
  21.9 3.2 %copy.40 = bf16[32,20,2048]{2,1,0:T(8,128)(2,1)} copy(bf16[32,20,2048]{2,0,1:T(8,128)(2,1)S(1)} %convolution_convert_fusion) | data formatting | bytes 5242880 | tf_op jit(solution)/shard_map/convert_element_type | solution.py:80
  25.1 0.0 all-to-all-done
  25.1 7.4 %all-to-all-start.1 = ((bf16[32,20,2048]{2,1,0:T(8,128)(2,1)}), bf16[32,20,2048]{2,1,0:T(8,128)(2,1)}, u32[]{:S(2)}, u32[]{:S(2)}) async-start(bf16[32,20,2048]{2,1,0:T(8,128)(2,1)} %copy.40), calls=%async_computation.1 | async-start | bytes 6291456 | tf_op jit(solution)/shard_map/all_to_all | solution.py:81
  32.6 86.2 %all-gather.3.cloned.1.call-done = bf16[4096,1280]{1,0:T(8,128)(2,1)} async-done(((bf16[256,1280]{1,0:T(8,128)(2,1)}), bf16[4096,1280]{1,0:T(8,128)(2,1)}) %all-gather.3.cloned.1.call-update) | async-done | bytes 10485776 | tf_op jit(solution)/shard_map/all_gather | solution.py:59
  118.7 0.8 collective-permute-start.4
  119.6 0.1 copy.39
  119.7 0.0 all-to-all-done.1
  119.7 5.7 %bitcast_convert_fusion = bf16[512,2048]{1,0:T(8,128)(2,1)} fusion(bf16[32,20,2048]{2,1,0:T(8,128)(2,1)} %all-to-all-done.1, s32[32,20]{0,1:T(8,128)S(1)} %copy.39), kind=kOutput, calls=%fused_computation.21 | convolution fusion | flops 1343553536 | bytes 4721152 | tf_op jit(solution)/shard_map/rps,psf->rf/dot_general | solution.py:84
  125.4 1.2 collective-permute-start
  126.6 1.5 collective-permute-start.2
  128.1 0.7 sort.17
  128.8 0.1 slice_compare_fusion
  128.9 0.1 add_select_fusion.2
  129.0 45.0 %collective-permute-done = bf16[512,2048]{1,0:T(8,128)(2,1)S(1)} collective-permute-done((bf16[512,2048]{1,0:T(8,128)(2,1)}, bf16[512,2048]{1,0:T(8,128)(2,1)S(1)}, u32[]{:S(2)}, u32[]{:S(2)}) %collective-permute-start) | collective-permute-done | bytes 2097184 | tf_op jit(solution)/shard_map/ppermute | solution.py:94
  174.0 0.1 slice.77
  174.1 0.2 collective-permute-start.1
  174.2 0.0 collective-permute-done.2
  174.3 2.8 slice.78
  177.0 2.1 collective-permute-start.3
  179.1 0.3 reduce-window.19
  179.5 0.1 slice.55
  179.6 0.1 slice_reduce_fusion.1
  179.7 0.1 fusion.65
  179.8 0.2 fusion.40
  180.0 2.0 multiply_cosine_fusion
  182.0 17.4 %collective-permute-done.1 = bf16[512,1024]{1,0:T(8,128)(2,1)} collective-permute-done((bf16[512,1024]{1,0:T(8,128)(2,1)S(1)}, bf16[512,1024]{1,0:T(8,128)(2,1)}, u32[]{:S(2)}, u32[]{:S(2)}) %collective-permute-start.1) | collective-permute-done | bytes 1048608 | tf_op jit(solution)/shard_map/ppermute | solution.py:96
  199.3 1.9 collective-permute-done.3
  201.2 1.9 maximum_bitcast_fusion
  203.1 0.3 copy-done.5
  203.4 3.3 %pad_maximum_fusion = bf16[4,512,2048]{2,1,0:T(8,128)(2,1)S(1)} fusion(bf16[1,512,2048]{2,1,0:T(8,128)(2,1)} %bitcast.9, bf16[1,512,2048]{2,1,0:T(8,128)(2,1)S(1)} %maximum_bitcast_fusion, bf16[1,512,2048]{2,1,0:T(8,128)(2,1)S(1)} %bitcast.105, bf16[1,512,2048]{2,1,0:T(8,128)(2,1)} %bitcast.6), kind=kLoop, calls=%fused_computation.8 | loop fusion | flops 12582912 | bytes 16777216 | tf_op jit(solution)/shard_map/stack | solution.py:100
  206.8 3.7 %fusion.73 = (bf16[4,512,1024]{2,1,0:T(8,128)(2,1)}, bf16[4,512,1024]{2,1,0:T(8,128)(2,1)}) fusion(bf16[4,512,2048]{2,1,0:T(8,128)(2,1)S(1)} %pad_maximum_fusion), kind=kLoop, calls=%fused_computation.120 | loop fusion | bytes 16777216 | tf_op jit(solution)/shard_map/jit(_take)/gather | solution.py:103
  210.5 5.0 %gather_fusion = bf16[4,512,1024]{2,1,0:T(8,128)(2,1)} fusion(bf16[4,512,1024]{2,1,0:T(8,128)(2,1)} %get-tuple-element.21, s32[1024]{0:T(1024)S(1)} %pad_clamp_fusion), kind=kCustom, calls=%fused_computation | custom fusion | bytes 8388624 | tf_op jit(solution)/shard_map/jit(_take)/gather | solution.py:103
  215.5 4.9 %gather_fusion.1 = bf16[4,512,1024]{2,1,0:T(8,128)(2,1)} fusion(bf16[4,512,1024]{2,1,0:T(8,128)(2,1)} %get-tuple-element.22, s32[1024]{0:T(1024)S(1)} %pad_clamp_fusion), kind=kCustom, calls=%fused_computation.1 | custom fusion | bytes 8388624 | tf_op jit(solution)/shard_map/jit(_take)/gather | solution.py:103
  220.4 6.6 %fusion = f32[512]{0:T(512)S(1)} fusion(bf16[4,512,1024]{2,1,0:T(8,128)(2,1)} %gather_fusion.1, bf16[4,512,1024]{2,1,0:T(8,128)(2,1)} %gather_fusion, pred[4]{0:T(512)(128)(4,1)S(1)} %compare_and_fusion), kind=kLoop, calls=%fused_computation.4 | loop fusion | flops 33553920 | bytes 8390660 | tf_op jit(solution)/shard_map/reduce_sum | solution.py:105
  227.1 5.0 %fusion.3 = bf16[512,4,2048]{2,0,1:T(8,128)(2,1)} fusion(f32[4,2048]{1,0:T(4,128)S(1)} %mul.123, f32[512]{0:T(512)S(1)} %add_rsqrt_fusion, bf16[4,512,1024]{2,1,0:T(8,128)(2,1)S(1)} %copy-done.3, bf16[4,512,1024]{2,1,0:T(8,128)(2,1)S(1)} %copy-done.2, pred[4]{0:T(512)(128)(4,1)S(1)} %compare_and_fusion), kind=kLoop, calls=%fused_computation.7 | loop fusion | flops 37748736 | bytes 16812036 | tf_op jit(solution)/shard_map/mul | solution.py:107
  232.1 11.4 %copy.42 = bf16[512,4,2048]{0,2,1:T(8,128)(2,1)} copy(bf16[512,4,2048]{2,0,1:T(8,128)(2,1)} %fusion.3) | data formatting | bytes 16777216 | tf_op jit(solution)/shard_map/mul | solution.py:107
  243.6 7.7 %constant_dynamic-slice_fusion = (bf16[512,16,1,256]{0,3,2,1:T(8,128)(2,1)}, bf16[512,16,1,256]{0,3,2,1:T(8,128)(2,1)}) fusion(bf16[512,16,2,256]{0,3,2,1:T(8,128)(2,1)} %bitcast.103, s32[]{:T(128)S(6)} %select_n.70, s32[]{:T(128)S(6)} %select_n.68), kind=kLoop, calls=%fused_computation.113 | loop fusion | bytes 16777224 | tf_op jit(solution)/shard_map/jit(_take) | solution.py:111
  251.2 6.4 %copy.53 = bf16[512,16,1,256]{3,0,1,2:T(8,128)(2,1)} copy(bf16[512,16,1,256]{0,3,2,1:T(8,128)(2,1)} %get-tuple-element.20) | data formatting | bytes 8388608
  257.6 6.4 %copy.54 = bf16[512,16,1,256]{3,0,1,2:T(8,128)(2,1)} copy(bf16[512,16,1,256]{0,3,2,1:T(8,128)(2,1)} %get-tuple-element.19) | data formatting | bytes 8388608
  264.0 10.7 %fusion.17 = f32[512,1280]{1,0:T(8,128)S(1)} fusion(bf16[16,256,1280]{2,1,0:T(8,128)(2,1)} %bitcast.110, bf16[512,16,1,256]{3,0,1,2:T(8,128)(2,1)} %copy.53, pred[]{:T(512)S(6)} %and.62), kind=kOutput, calls=%fused_computation.27 | convolution fusion | flops 5370806272 | bytes 17301504 | tf_op jit(solution)/shard_map/rhj,hjn->rn/dot_general | solution.py:112
  274.7 0.0 copy-start.11
  274.8 9.4 %fusion.23 = f32[512,1280]{1,0:T(8,128)S(1)} fusion(f32[512,1280]{1,0:T(8,128)S(1)} %fusion.17, bf16[16,256,1280]{2,1,0:T(8,128)(2,1)} %collective-permute-done.4, bf16[512,16,1,256]{3,0,1,2:T(8,128)(2,1)S(1)} %copy-done.6, pred[]{:T(512)S(6)} %and.63), kind=kOutput, calls=%fused_computation.29 | convolution fusion | flops 5371461632 | bytes 19922944 | tf_op jit(solution)/shard_map/rhj,hjn->rn/dot_general | solution.py:114
  284.2 0.3 fusion.27
  284.5 0.5 copy.58
  285.0 0.0 copy-start.12
  285.0 0.7 fusion.74
  285.8 1.4 fusion.60
  287.2 0.8 subtract_convert_fusion
  288.0 2.2 fusion.5
  290.3 0.0 copy-start.13
  290.3 1.7 fusion.4
  292.0 0.0 copy-start.1
  292.0 2.7 fusion.32
  294.7 1.3 copy.49
  (41 shorter events, 0.2 us)
Async XLA Ops:
  6.5 13.9 %copy-start = (bf16[512,2048]{1,0:T(8,128)(2,1)S(1)}, bf16[512,2048]{1,0:T(8,128)(2,1)}, u32[]{:S(2)}) copy-start(bf16[512,2048]{1,0:T(8,128)(2,1)} %param.12) | copy-start | bytes 6291460
  6.5 112.2 %all-gather.3.cloned.1.call-start = ((), (), s32[]{:S(2)}) async-start(), calls=%async_computation.2 | async-start | bytes 11141120 | tf_op jit(solution)/shard_map/all_gather | solution.py:59
  12.1 13.0 %all-to-all-start = ((s32[32,1,20]{2,1,0:T(1,128)}), s32[32,1,20]{2,1,0:T(1,128)S(1)}, u32[]{:S(2)}, u32[]{:S(2)}) async-start(s32[32,1,20]{2,1,0:T(1,128)} %copy.38), calls=%async_computation | async-start | bytes 32768 | tf_op jit(solution)/shard_map/all_to_all | solution.py:74
  25.1 94.5 %all-to-all-start.1 = ((bf16[32,20,2048]{2,1,0:T(8,128)(2,1)}), bf16[32,20,2048]{2,1,0:T(8,128)(2,1)}, u32[]{:S(2)}, u32[]{:S(2)}) async-start(bf16[32,20,2048]{2,1,0:T(8,128)(2,1)} %copy.40), calls=%async_computation.1 | async-start | bytes 6291456 | tf_op jit(solution)/shard_map/all_to_all | solution.py:81
  118.7 156.0 %collective-permute-start.4 = (bf16[16,256,1280]{2,1,0:T(8,128)(2,1)}, bf16[16,256,1280]{2,1,0:T(8,128)(2,1)}, u32[]{:S(2)}, u32[]{:S(2)}) collective-permute-start(bf16[16,256,1280]{2,1,0:T(8,128)(2,1)} %bitcast.109), channel_id=1, source_target_pairs={{0,4},{4,0},{1,5},{5,1},{2,6},{6,2},{3,7},{7,3},{8,12},{12,8},{9,1... | collective-permute-start | bytes 31457288 | tf_op jit(solution)/shard_map/ppermute | solution.py:60
  119.7 9.2 %copy-start.9 = (s32[512]{0:T(512)S(1)}, s32[512]{0:T(512)}, u32[]{:S(2)}) copy-start(s32[512]{0:T(512)} %param.14) | copy-start | bytes 6148
  125.4 53.7 %copy-start.10 = (f32[8192]{0:T(1024)S(1)}, f32[8192]{0:T(1024)}, u32[]{:S(2)}) copy-start(f32[8192]{0:T(1024)} %param.15) | copy-start | bytes 98308
  125.4 48.6 %collective-permute-start = (bf16[512,2048]{1,0:T(8,128)(2,1)}, bf16[512,2048]{1,0:T(8,128)(2,1)S(1)}, u32[]{:S(2)}, u32[]{:S(2)}) collective-permute-start(bf16[512,2048]{1,0:T(8,128)(2,1)} %bitcast_convert_fusion), channel_id=1, source_target_pairs={{0,1},{1,2},{2,3},{3,0},{4,5},{5,6},{6,7},{7,4},{8,9},{9,10},{10,1... | collective-permute-start | bytes 6291464 | tf_op jit(solution)/shard_map/ppermute | solution.py:94
  126.6 47.7 %collective-permute-start.2 = (bf16[512,2048]{1,0:T(8,128)(2,1)}, bf16[512,2048]{1,0:T(8,128)(2,1)}, u32[]{:S(2)}, u32[]{:S(2)}) collective-permute-start(bf16[512,2048]{1,0:T(8,128)(2,1)} %bitcast_convert_fusion), channel_id=1, source_target_pairs={{0,3},{1,0},{2,1},{3,2},{4,7},{5,4},{6,5},{7,6},{8,11},{9,8},{10,9... | collective-permute-start | bytes 6291464 | tf_op jit(solution)/shard_map/ppermute | solution.py:95
  174.0 25.3 %copy-start.4 = (bf16[512,2048]{1,0:T(8,128)(2,1)}, bf16[512,2048]{1,0:T(8,128)(2,1)S(1)}, u32[]{:S(2)}) copy-start(bf16[512,2048]{1,0:T(8,128)(2,1)S(1)} %collective-permute-done) | copy-start | bytes 6291460
  174.1 25.2 %collective-permute-start.1 = (bf16[512,1024]{1,0:T(8,128)(2,1)S(1)}, bf16[512,1024]{1,0:T(8,128)(2,1)}, u32[]{:S(2)}, u32[]{:S(2)}) collective-permute-start(bf16[512,1024]{1,0:T(8,128)(2,1)S(1)} %slice.77), channel_id=1, source_target_pairs={{0,1},{1,2},{2,3},{3,0},{4,5},{5,6},{6,7},{7,4},{8,9},{9,10},{10,1... | collective-permute-start | bytes 3145736 | tf_op jit(solution)/shard_map/ppermute | solution.py:96
  177.0 24.2 %collective-permute-start.3 = (bf16[512,1024]{1,0:T(8,128)(2,1)}, bf16[512,1024]{1,0:T(8,128)(2,1)}, u32[]{:S(2)}, u32[]{:S(2)}) collective-permute-start(bf16[512,1024]{1,0:T(8,128)(2,1)} %slice.78), channel_id=1, source_target_pairs={{0,3},{1,0},{2,1},{3,2},{4,7},{5,4},{6,5},{7,6},{8,11},{9,8},{10,9... | collective-permute-start | bytes 3145736 | tf_op jit(solution)/shard_map/ppermute | solution.py:97
  201.2 2.2 copy-start.5
  220.4 6.7 %copy-start.2 = (bf16[4,512,1024]{2,1,0:T(8,128)(2,1)S(1)}, bf16[4,512,1024]{2,1,0:T(8,128)(2,1)}, u32[]{:S(2)}) copy-start(bf16[4,512,1024]{2,1,0:T(8,128)(2,1)} %gather_fusion) | copy-start | bytes 12582916
  220.4 6.7 %copy-start.3 = (bf16[4,512,1024]{2,1,0:T(8,128)(2,1)S(1)}, bf16[4,512,1024]{2,1,0:T(8,128)(2,1)}, u32[]{:S(2)}) copy-start(bf16[4,512,1024]{2,1,0:T(8,128)(2,1)} %gather_fusion.1) | copy-start | bytes 12582916
  264.0 10.8 %copy-start.6 = (bf16[512,16,1,256]{3,0,1,2:T(8,128)(2,1)S(1)}, bf16[512,16,1,256]{3,0,1,2:T(8,128)(2,1)}, u32[]{:S(2)}) copy-start(bf16[512,16,1,256]{3,0,1,2:T(8,128)(2,1)} %copy.54) | copy-start | bytes 12582916
  274.7 9.5 %copy-start.11 = (f32[1024]{0:T(1024)S(1)}, f32[1024]{0:T(1024)}, u32[]{:S(2)}) copy-start(f32[1024]{0:T(1024)} %param.19) | copy-start | bytes 12292
  285.0 0.7 copy-start.12
  285.0 2.2 copy-start.7
  285.0 2.2 copy-start.8
  290.3 1.8 copy-start.13
  292.0 4.0 %copy-start.1 = (bf16[512,2048]{1,0:T(8,128)(2,1)S(1)}, bf16[512,2048]{1,0:T(8,128)(2,1)}, u32[]{:S(2)}) copy-start(bf16[512,2048]{1,0:T(8,128)(2,1)} %param.12) | copy-start | bytes 6291460
Sparse Core Ops, SparseCore 0:
  9.5 109.1 all-gather.2

commit v3 on v2

--- a/solution.py
+++ b/solution.py
@@ -70,21 +70,31 @@
         slot_hits = (target[None, None, :] == jnp.arange(peer_count, dtype=jnp.int32)[:, None, None]) & (
             ranking[None, None, :] == jnp.arange(slots_each, dtype=jnp.int32)[None, :, None]
         )
-        parcels = jnp.sum(jnp.where(slot_hits, learner_slot[None, None, :] + 1, 0), axis=2) - 1
-        labels = lax.all_to_all(parcels, SEQ, split_axis=0, concat_axis=0, tiled=True)
+        tagged = jnp.sum(jnp.where(slot_hits, learner_slot[None, None, :] + 1, 0), axis=2)
+        tag_row = jnp.concatenate(
+            [
+                (tagged // 32).astype(jnp.bfloat16),
+                (tagged % 32).astype(jnp.bfloat16),
+                jnp.zeros((peer_count, width - 2 * slots_each), jnp.bfloat16),
+            ],
+            axis=1,
+        )
         picked = jnp.einsum(
             "psr,rf->psf",
             slot_hits.astype(jnp.bfloat16),
             rollout_rows,
             preferred_element_type=jnp.float32,
         ).astype(jnp.bfloat16)
-        arrived = lax.all_to_all(picked, SEQ, split_axis=0, concat_axis=0, tiled=True)
+        payload = jnp.concatenate([picked, tag_row[:, None, :]], axis=1)
+        arrived = lax.all_to_all(payload, SEQ, split_axis=0, concat_axis=0, tiled=True)
+        tags = arrived[:, slots_each, : 2 * slots_each].astype(jnp.int32)
+        labels = tags[:, :slots_each] * 32 + tags[:, slots_each:] - 1
         row_numbers = jnp.arange(row_count, dtype=jnp.int32)
         label_hits = labels[None, :, :] == row_numbers[:, None, None]
         learner_part = jnp.einsum(
             "rps,psf->rf",
             label_hits.astype(jnp.bfloat16),
-            arrived,
+            arrived[:, :slots_each, :],
             preferred_element_type=jnp.float32,
         ).astype(jnp.bfloat16)
 
@@ -96,22 +106,29 @@
         far_a = lax.ppermute(from_left[:, :half], TP, to_right)
         far_b = lax.ppermute(from_right[:, half:], TP, to_left)
         far = jnp.concatenate([far_a, far_b], axis=1)
+        pieces = [learner_part, from_left, far, from_right]
         tp_index = lax.axis_index(TP)
-        by_offset = jnp.stack([learner_part, from_left, far, from_right])
-        order = (tp_index - jnp.arange(tp_count, dtype=jnp.int32)) % tp_count
-        inverse = jnp.argsort(order)
-        quarters = jnp.take(by_offset, inverse, axis=0)
-        widened = quarters.astype(jnp.float32)
-        mean_sq = jnp.sum(widened * widened, axis=(0, 2), keepdims=True) / (width * tp_count)
-        gain = norm_gain.reshape(tp_count, 1, width)
-        normed = (widened * lax.rsqrt(mean_sq + EPS) * gain).astype(jnp.bfloat16)
-        normed = normed.transpose(1, 0, 2).reshape(row_count, chip_count, core_count, depth)
+        wide = [p.astype(jnp.float32) for p in pieces]
+        total_sq = sum(jnp.sum(w * w, axis=-1, keepdims=True) for w in wide)
+        scale = lax.rsqrt(total_sq / (width * tp_count) + EPS)
+        normed = []
+        for k, w in enumerate(wide):
+            quarter = (tp_index - k) % tp_count
+            gain = lax.dynamic_slice_in_dim(norm_gain, quarter * width, width)
+            normed.append((w * scale * gain).astype(jnp.bfloat16))
+
         core_index = lax.axis_index(CORE)
-        own_cols = jnp.take(normed, core_index, axis=2)
-        other_cols = jnp.take(normed, (core_index + 1) % core_count, axis=2)
-        projected = jnp.einsum(
-            "rhj,hjn->rn", own_cols, own_weights, preferred_element_type=jnp.float32
-        ) + jnp.einsum("rhj,hjn->rn", other_cols, other_weights, preferred_element_type=jnp.float32)
+        natural = jnp.where(
+          core_index == 0,
+          jnp.stack([own_weights, other_weights], axis=1),
+          jnp.stack([other_weights, own_weights], axis=1),
+        ).reshape(chip_count * core_count * depth, own_weights.shape[-1])
+        projected = None
+        for k, piece in enumerate(normed):
+            quarter = (tp_index - k) % tp_count
+            rows = lax.dynamic_slice_in_dim(natural, quarter * width, width, axis=0)
+            part = jnp.dot(piece, rows, preferred_element_type=jnp.float32)
+            projected = part if projected is None else projected + part
         queries = projected[:, :q_cols]
         key_proj = projected[:, q_cols : q_cols + k_cols]
         value_proj = projected[:, q_cols + k_cols :]

time: 308 us -> 286 us (0.929)
  local copies, waits for them, and re-layouts: 55.6 us -> 7.84 us
  blocking collectives: 0 us -> 43.6 us
  starting transfers between devices: 21.5 us -> 7 us
    ppermute x1, waiting for transfers between devices: 45 us -> 0.01 us  [body(): from_left = lax.ppermute(learner_part, TP, to_right)]
    ppermute x1, waiting for transfers between devices: 0.01 us -> 44.7 us  [body(): from_right = lax.ppermute(learner_part, TP, to_left)]
    all_to_all x0 -> x1, blocking collectives: none -> 43.6 us  [body(): lax.all_to_all(payload, SEQ, split_axis=0, concat_axis=0, tiled=True)]
    select_n x2, other arithmetic: 0.01 us -> 16.3 us  [the longest x1 15.6 us: body(): jnp.where(core_index == 0, jnp.stack([own_weights, other_weights], axis=1...]
    ppermute x1, waiting for transfers between devices: 1.86 us -> 17.8 us  [body(): far_b = lax.ppermute(from_right[:, half:], TP, to_left)]
    all_to_all x2 -> x0, starting transfers between devices: 15.7 us -> none  [the longest x1 8.27 us: body(): lax.all_to_all(parcels, SEQ, split_axis=0, concat_axis=0, tiled=True)]
    ppermute x1, waiting for transfers between devices: 17.4 us -> 3.48 us  [body(): far_a = lax.ppermute(from_left[:, :half], TP, to_right)]
    gather x3 -> x0, local copies, waits for them, and re-layouts: 13.6 us -> none  [body(): quarters = jnp.take(by_offset, inverse, axis=0)]
  transfers between devices with their start and end apart: 8 -> 6, of which waited for: 4 -> 4; matrix products, arithmetic and copies ran while one was open for 31% -> 7% of each run, Pallas kernels for 0% -> 0%
where the time goes in v3:
time: 286 us; the launch traced here: 281 us
  waiting for transfers between devices  148 us (52%)
  blocking collectives  43.6 us (15%)
  matrix products  32.2 us (11%)
  other arithmetic  29.6 us (10%)
  between operations  13.7 us (5%)
  local copies, waits for them, and re-layouts  7.84 us (3%)
  starting transfers between devices  7 us (2%)
    all_gather x1, waiting for transfers between devices, body(): own_weights = lax.all_gather(weights, CHIPS, axis=0, tiled=False)  81.6 us
    ppermute x1, waiting for transfers between devices, body(): from_right = lax.ppermute(learner_part, TP, to_left)  44.7 us
    all_to_all x1, blocking collectives, body(): lax.all_to_all(payload, SEQ, split_axis=0, concat_axis=0, tiled=True)  43.6 us
    dot_general x4, matrix products, body(): part = jnp.dot(piece, rows, preferred_element_type=jnp.float32)  19.9 us
    ppermute x1, waiting for transfers between devices, body(): far_b = lax.ppermute(from_right[:, half:], TP, to_left)  17.8 us
    select_n x1, other arithmetic, body(): jnp.where(core_index == 0, jnp.stack([own_weights, other_weights], axis=1...  15.6 us
    dot_general x1, matrix products, body(): jnp.einsum('rps,psf->rf', label_hits.astype(jnp.bfloat16), arrived[:, :sl...  5.9 us
  transfers between devices with their start and end apart: 6, of which 4 were waited for; matrix products, arithmetic and copies ran while one was open for 7% of the time, Pallas kernels for 0%

profile of v3, /device:TPU:49, one launch (start us, length us, event | category | flops | bytes accessed | tf_op | source)
XLA Modules:
  0.0 281.4 jit_solution(5926761540051477145)
XLA Ops:
  6.5 0.0 copy-start
  6.5 0.0 all-gather.3.cloned.1.call-start
  6.5 2.1 pad_maximum_fusion.3
  8.7 0.0 all-gather.3.cloned.1.call-update
  8.7 81.6 %all-gather.3.cloned.1.call-done = bf16[4096,1280]{1,0:T(8,128)(2,1)} async-done(((bf16[256,1280]{1,0:T(8,128)(2,1)}), bf16[4096,1280]{1,0:T(8,128)(2,1)}) %all-gather.3.cloned.1.call-update) | async-done | bytes 10485776 | tf_op jit(solution)/shard_map/all_gather | solution.py:59
  90.3 0.8 collective-permute-start.4
  91.1 0.7 add_select_fusion.3
  91.8 1.2 reduce-window.15
  93.0 0.2 slice_reduce_fusion
  93.2 0.1 fusion.80
  93.4 0.4 fusion.53
  93.8 0.1 copy.25
  94.0 0.1 concatenate.34
  94.1 0.0 copy-done
  94.1 1.5 convolution_convert_fusion
  95.7 0.2 pad_maximum_fusion
  95.9 1.5 copy.29
  97.4 43.6 %all_to_all.5 = bf16[32,21,2048]{2,1,0:T(8,128)(2,1)S(1)} all-to-all(bf16[32,21,2048]{2,1,0:T(8,128)(2,1)S(1)} %copy.29), channel_id=1, replica_groups=mesh['chips'=16,'core'=2,'tp'=4] {'chips','core'}, dimensions={0} | all-to-all | bytes 5505024 | tf_op jit(solution)/shard_map/all_to_all | solution.py:89
  141.0 1.7 copy-done.2
  142.7 0.1 fusion.84
  142.8 0.1 copy.31
  142.9 5.9 %fusion.10 = (f32[512]{0:T(512)S(1)}, bf16[512,2048]{1,0:T(8,128)(2,1)}) fusion(bf16[32,20,2048]{2,1,0:T(8,128)(2,1)} %bitcast.89, s32[32,20]{0,1:T(8,128)S(1)} %copy.31), kind=kOutput, calls=%fused_computation.22 | convolution fusion | flops 1346698752 | bytes 4723200 | tf_op jit(solution)/shard_map/rps,psf->rf/dot_general | solution.py:94
  148.8 2.4 collective-permute-start.2
  151.2 0.0 collective-permute-start
  151.2 0.0 copy-done.3
  151.2 0.1 slice_compare_fusion
  151.3 0.1 add_select_fusion.4
  151.4 0.3 reduce-window.19
  151.7 0.1 slice.71
  151.8 0.1 slice_reduce_fusion.1
  151.9 0.0 copy-done.4
  151.9 0.1 fusion.89
  152.0 44.7 %collective-permute-done.2 = bf16[512,2048]{1,0:T(8,128)(2,1)} collective-permute-done((bf16[512,2048]{1,0:T(8,128)(2,1)}, bf16[512,2048]{1,0:T(8,128)(2,1)}, u32[]{:S(2)}, u32[]{:S(2)}) %collective-permute-start.2) | collective-permute-done | bytes 2097184 | tf_op jit(solution)/shard_map/ppermute | solution.py:105
  196.7 1.3 slice.83
  198.0 3.5 %collective-permute-start.3 = (bf16[512,1024]{1,0:T(8,128)(2,1)S(1)}, bf16[512,1024]{1,0:T(8,128)(2,1)S(1)}, u32[]{:S(2)}, u32[]{:S(2)}) collective-permute-start(bf16[512,1024]{1,0:T(8,128)(2,1)S(1)} %slice.83), channel_id=1, source_target_pairs={{0,3},{1,0},{2,1},{3,2},{4,7},{5,4},{6,5},{7,6},{8,11},{9,8},{10,9... | collective-permute-start | bytes 3145736 | tf_op jit(solution)/shard_map/ppermute | solution.py:107
  201.5 0.0 collective-permute-done
  201.5 0.1 slice.82
  201.6 0.3 collective-permute-start.1
  201.9 0.2 fusion.58
  202.1 1.0 multiply_cosine_fusion
  203.1 2.1 fusion.19
  205.2 0.5 fusion.13
  205.7 17.8 %collective-permute-done.3 = bf16[512,1024]{1,0:T(8,128)(2,1)S(1)} collective-permute-done((bf16[512,1024]{1,0:T(8,128)(2,1)S(1)}, bf16[512,1024]{1,0:T(8,128)(2,1)S(1)}, u32[]{:S(2)}, u32[]{:S(2)}) %collective-permute-start.3) | collective-permute-done | bytes 1048608 | tf_op jit(solution)/shard_map/ppermute | solution.py:107
  223.4 3.5 %collective-permute-done.1 = bf16[512,1024]{1,0:T(8,128)(2,1)S(1)} collective-permute-done((bf16[512,1024]{1,0:T(8,128)(2,1)S(1)}, bf16[512,1024]{1,0:T(8,128)(2,1)S(1)}, u32[]{:S(2)}, u32[]{:S(2)}) %collective-permute-start.1) | collective-permute-done | bytes 1048608 | tf_op jit(solution)/shard_map/ppermute | solution.py:106
  226.9 0.5 fusion.16
  227.4 0.0 collective-permute-done.4
  227.4 15.6 %maximum_select_fusion = bf16[16,2,256,1280]{3,2,1,0:T(8,128)(2,1)S(1)} fusion(bf16[16,1,256,1280]{3,2,1,0:T(8,128)(2,1)} %bitcast.9, bf16[16,1,256,1280]{3,2,1,0:T(8,128)(2,1)} %bitcast.88, pred[]{:T(512)S(6)} %eq.121), kind=kLoop, calls=%fused_computation | loop fusion | flops 31457280 | bytes 41943040 | tf_op jit(solution)/shard_map/jit(_where)/select_n | solution.py:121
  243.0 4.6 %fusion.2 = f32[512,1280]{1,0:T(8,128)S(1)} fusion(bf16[8192,1280]{1,0:T(8,128)(2,1)S(1)} %bitcast.82, s32[]{:T(128)S(6)} %select_n.104, bf16[512,2048]{1,0:T(8,128)(2,1)} %collective-permute-done.2, f32[2048]{0:T(1024)S(1)} %get-tuple-element.13, f32[512]{0:T(512)S(1)} %add_rsqrt_fusion), kind=kOutput, calls=%fused_computation.14 | convolution fusion | flops 2688548864 | bytes 9971716 | tf_op jit(solution)/shard_map/dot_general | solution.py:130
  247.6 4.5 %fusion.4 = f32[512,1280]{1,0:T(8,128)} fusion(bf16[8192,1280]{1,0:T(8,128)(2,1)S(1)} %bitcast.83, s32[]{:T(128)S(6)} %select_n.102, f32[2048]{0:T(1024)S(1)} %get-tuple-element.14, f32[512]{0:T(512)S(1)} %add_rsqrt_fusion, bf16[512,1024]{1,0:T(8,128)(2,1)S(1)} %collective-permute-done.3, bf16[512,1024]{1,0:T(8,128)(2,1)S(1)} %collective-permute-done.1), kind=kOutput, calls=%fused_computation.16 | convolution fusion | flops 2691694592 | bytes 9971716 | tf_op jit(solution)/shard_map/dot_general | solution.py:130
  252.0 4.5 %fusion.6 = f32[512,1280]{1,0:T(8,128)} fusion(bf16[8192,1280]{1,0:T(8,128)(2,1)S(1)} %bitcast.84, s32[]{:T(128)S(6)} %select_n.100, bf16[512,2048]{1,0:T(8,128)(2,1)S(1)} %collective-permute-done, f32[2048]{0:T(1024)S(1)} %get-tuple-element.12, f32[512]{0:T(512)S(1)} %add_rsqrt_fusion), kind=kOutput, calls=%fused_computation.18 | convolution fusion | flops 2688548864 | bytes 9971716 | tf_op jit(solution)/shard_map/dot_general | solution.py:130
  256.5 6.3 %fusion.31 = f32[512,1280]{1,0:T(8,128)S(1)} fusion(f32[512,1280]{1,0:T(8,128)S(1)} %fusion.2, f32[512,1280]{1,0:T(8,128)} %fusion.4, f32[512,1280]{1,0:T(8,128)} %fusion.6, bf16[8192,1280]{1,0:T(8,128)(2,1)S(1)} %bitcast.85, s32[]{:T(128)S(6)} %select_n.95, bf16[512,2048]{1,0:T(8,128)(2,1)} %get-tuple-element.22, f32[2048]{0:T(1024)S(1)} %get-tuple-element.11, ...), kind=kOutput, calls=%fused_computation.40 | convolution fusion | flops 2690514944 | bytes 17836036 | tf_op jit(solution)/shard_map/dot_general | solution.py:130
  262.9 0.0 copy-done.5
  262.9 0.3 fusion.39
  263.2 0.5 copy.46
  263.6 0.0 copy-start.6
  263.6 0.7 fusion.99
  264.4 1.4 fusion.78
  265.8 0.8 subtract_convert_fusion
  266.6 2.2 fusion.1
  268.8 0.0 copy-start.7
  268.8 1.7 fusion
  270.6 0.0 copy-start.1
  270.6 2.7 fusion.50
  273.3 1.3 copy.37
  (21 shorter events, 0.3 us)
Async XLA Ops:
  6.5 87.6 %copy-start = (bf16[512,2048]{1,0:T(8,128)(2,1)S(1)}, bf16[512,2048]{1,0:T(8,128)(2,1)}, u32[]{:S(2)}) copy-start(bf16[512,2048]{1,0:T(8,128)(2,1)} %param.10) | copy-start | bytes 6291460
  6.5 83.7 %all-gather.3.cloned.1.call-start = ((), (), s32[]{:S(2)}) async-start(), calls=%async_computation.1 | async-start | bytes 11141120 | tf_op jit(solution)/shard_map/all_gather | solution.py:59
  90.3 137.1 %collective-permute-start.4 = (bf16[16,256,1280]{2,1,0:T(8,128)(2,1)}, bf16[16,256,1280]{2,1,0:T(8,128)(2,1)}, u32[]{:S(2)}, u32[]{:S(2)}) collective-permute-start(bf16[16,256,1280]{2,1,0:T(8,128)(2,1)} %bitcast.87), channel_id=1, source_target_pairs={{0,4},{4,0},{1,5},{5,1},{2,6},{6,2},{3,7},{7,3},{8,12},{12,8},{9,1... | collective-permute-start | bytes 31457288 | tf_op jit(solution)/shard_map/ppermute | solution.py:60
  141.0 1.7 copy-start.2
  142.9 8.3 %copy-start.3 = (s32[512]{0:T(512)S(1)}, s32[512]{0:T(512)}, u32[]{:S(2)}) copy-start(s32[512]{0:T(512)} %param.12) | copy-start | bytes 6148
  142.9 9.0 %copy-start.4 = (f32[8192]{0:T(1024)S(1)}, f32[8192]{0:T(1024)}, u32[]{:S(2)}) copy-start(f32[8192]{0:T(1024)} %param.13) | copy-start | bytes 98308
  148.8 48.0 %collective-permute-start.2 = (bf16[512,2048]{1,0:T(8,128)(2,1)}, bf16[512,2048]{1,0:T(8,128)(2,1)}, u32[]{:S(2)}, u32[]{:S(2)}) collective-permute-start(bf16[512,2048]{1,0:T(8,128)(2,1)} %get-tuple-element.22), channel_id=1, source_target_pairs={{0,3},{1,0},{2,1},{3,2},{4,7},{5,4},{6,5},{7,6},{8,11},{9,8},{10,9... | collective-permute-start | bytes 6291464 | tf_op jit(solution)/shard_map/ppermute | solution.py:105
  151.2 50.3 %collective-permute-start = (bf16[512,2048]{1,0:T(8,128)(2,1)}, bf16[512,2048]{1,0:T(8,128)(2,1)S(1)}, u32[]{:S(2)}, u32[]{:S(2)}) collective-permute-start(bf16[512,2048]{1,0:T(8,128)(2,1)} %get-tuple-element.22), channel_id=1, source_target_pairs={{0,1},{1,2},{2,3},{3,0},{4,5},{5,6},{6,7},{7,4},{8,9},{9,10},{10,1... | collective-permute-start | bytes 6291464 | tf_op jit(solution)/shard_map/ppermute | solution.py:104
  198.0 25.4 %collective-permute-start.3 = (bf16[512,1024]{1,0:T(8,128)(2,1)S(1)}, bf16[512,1024]{1,0:T(8,128)(2,1)S(1)}, u32[]{:S(2)}, u32[]{:S(2)}) collective-permute-start(bf16[512,1024]{1,0:T(8,128)(2,1)S(1)} %slice.83), channel_id=1, source_target_pairs={{0,3},{1,0},{2,1},{3,2},{4,7},{5,4},{6,5},{7,6},{8,11},{9,8},{10,9... | collective-permute-start | bytes 3145736 | tf_op jit(solution)/shard_map/ppermute | solution.py:107
  201.6 25.3 %collective-permute-start.1 = (bf16[512,1024]{1,0:T(8,128)(2,1)S(1)}, bf16[512,1024]{1,0:T(8,128)(2,1)S(1)}, u32[]{:S(2)}, u32[]{:S(2)}) collective-permute-start(bf16[512,1024]{1,0:T(8,128)(2,1)S(1)} %slice.82), channel_id=1, source_target_pairs={{0,1},{1,2},{2,3},{3,0},{4,5},{5,6},{6,7},{7,4},{8,9},{9,10},{10,1... | collective-permute-start | bytes 3145736 | tf_op jit(solution)/shard_map/ppermute | solution.py:106
  256.5 6.4 %copy-start.5 = (f32[1024]{0:T(1024)S(1)}, f32[1024]{0:T(1024)}, u32[]{:S(2)}) copy-start(f32[1024]{0:T(1024)} %param.17) | copy-start | bytes 12292
  263.6 0.7 copy-start.6
  268.8 1.7 copy-start.7
  270.6 4.0 %copy-start.1 = (bf16[512,2048]{1,0:T(8,128)(2,1)S(1)}, bf16[512,2048]{1,0:T(8,128)(2,1)}, u32[]{:S(2)}) copy-start(bf16[512,2048]{1,0:T(8,128)(2,1)} %param.10) | copy-start | bytes 6291460
Sparse Core Ops, SparseCore 0:
  9.5 80.6 all-gather.2

commit v4 on v3

--- a/solution.py
+++ b/solution.py
@@ -53,7 +53,7 @@
         slots_each = row_count // peer_count + row_count // (4 * peer_count)
         q_cols = q_weight.shape[1]
         k_cols = k_weight.shape[1]
-        depth = q_weight.shape[0]
+
 
         weights = jnp.concatenate([q_weight, k_weight, v_weight], axis=1)
         own_weights = lax.all_gather(weights, CHIPS, axis=0, tiled=False)
@@ -98,6 +98,19 @@
             preferred_element_type=jnp.float32,
         ).astype(jnp.bfloat16)
 
+        tp_index = lax.axis_index(TP)
+        core_index = lax.axis_index(CORE)
+        wide = learner_part.astype(jnp.float32)
+        own_sq = jnp.sum(wide * wide, axis=-1)
+        others = [
+            lax.ppermute(own_sq, TP, [(t, (t + k) % tp_count) for t in range(tp_count)])
+            for k in range(1, tp_count)
+        ]
+        total_sq = own_sq
+        for other in others:
+            total_sq = total_sq + other
+        scale = lax.rsqrt(total_sq / (width * tp_count) + EPS)[:, None]
+
         to_right = [(t, (t + 1) % tp_count) for t in range(tp_count)]
         to_left = [(t, (t - 1) % tp_count) for t in range(tp_count)]
         half = width // 2
@@ -107,28 +120,32 @@
         far_b = lax.ppermute(from_right[:, half:], TP, to_left)
         far = jnp.concatenate([far_a, far_b], axis=1)
         pieces = [learner_part, from_left, far, from_right]
-        tp_index = lax.axis_index(TP)
-        wide = [p.astype(jnp.float32) for p in pieces]
-        total_sq = sum(jnp.sum(w * w, axis=-1, keepdims=True) for w in wide)
-        scale = lax.rsqrt(total_sq / (width * tp_count) + EPS)
-        normed = []
-        for k, w in enumerate(wide):
+
+        block = width // (4 * core_count)
+        span = 4 * block
+        own_rows = own_weights.reshape(tp_count, span, own_weights.shape[-1])
+        other_rows = other_weights.reshape(tp_count, span, own_weights.shape[-1])
+
+        def core_block(x, c):
+            return jnp.concatenate(
+                [x[:, (hl * core_count + c) * block : (hl * core_count + c + 1) * block] for hl in range(4)],
+                axis=1,
+            )
+
+        projected = None
+        for k in (0, 1, 3, 2):
+            piece = pieces[k]
             quarter = (tp_index - k) % tp_count
             gain = lax.dynamic_slice_in_dim(norm_gain, quarter * width, width)
-            normed.append((w * scale * gain).astype(jnp.bfloat16))
-
-        core_index = lax.axis_index(CORE)
-        natural = jnp.where(
-          core_index == 0,
-          jnp.stack([own_weights, other_weights], axis=1),
-          jnp.stack([other_weights, own_weights], axis=1),
-        ).reshape(chip_count * core_count * depth, own_weights.shape[-1])
-        projected = None
-        for k, piece in enumerate(normed):
-            quarter = (tp_index - k) % tp_count
-            rows = lax.dynamic_slice_in_dim(natural, quarter * width, width, axis=0)
-            part = jnp.dot(piece, rows, preferred_element_type=jnp.float32)
-            projected = part if projected is None else projected + part
+            normed = (piece.astype(jnp.float32) * scale * gain).astype(jnp.bfloat16)
+            first = core_block(normed, 0)
+            second = core_block(normed, 1)
+            mine = jnp.where(core_index == 0, first, second)
+            theirs = jnp.where(core_index == 0, second, first)
+            for cols, rows_of in ((mine, own_rows), (theirs, other_rows)):
+                rows = lax.dynamic_index_in_dim(rows_of, quarter, axis=0, keepdims=False)
+                part = jnp.dot(cols, rows, preferred_element_type=jnp.float32)
+                projected = part if projected is None else projected + part
         queries = projected[:, :q_cols]
         key_proj = projected[:, q_cols : q_cols + k_cols]
         value_proj = projected[:, q_cols + k_cols :]

time: 286 us -> 270 us (0.944)
  other arithmetic: 29.6 us -> 18.1 us
  waiting for transfers between devices: 148 us -> 141 us
    ppermute x1, waiting for transfers between devices: 0.01 us -> 45.5 us  [body(): from_left = lax.ppermute(learner_part, TP, to_right)]
    ppermute x1, waiting for transfers between devices: 44.7 us -> 0.01 us  [body(): from_right = lax.ppermute(learner_part, TP, to_left)]
    ppermute x0 -> x3, waiting for transfers between devices: none -> 19.4 us  [body(): lax.ppermute(own_sq, TP, [(t, (t + k) % tp_count) for t in range(tp_count)])]
    ppermute x1, waiting for transfers between devices: 17.8 us -> 0.01 us  [body(): far_b = lax.ppermute(from_right[:, half:], TP, to_left)]
    select_n x1 -> x0, other arithmetic: 15.6 us -> none  [body(): jnp.where(core_index == 0, jnp.stack([own_weights, other_weights], axis=1...]
    all_gather x1, waiting for transfers between devices: 81.6 us -> 75.7 us  [body(): own_weights = lax.all_gather(weights, CHIPS, axis=0, tiled=False)]
    convert_element_type x0 -> x1, other arithmetic: none -> 4.51 us  [body(): normed = (piece.astype(jnp.float32) * scale * gain).astype(jnp.bfloat16)]
    ppermute x1, waiting for transfers between devices: 3.48 us -> 0.01 us  [body(): far_a = lax.ppermute(from_left[:, :half], TP, to_right)]
  transfers between devices with their start and end apart: 6 -> 9, of which waited for: 4 -> 4; matrix products, arithmetic and copies ran while one was open for 7% -> 11% of each run, Pallas kernels for 0% -> 0%
where the time goes in v4:
time: 270 us; the launch traced here: 265 us
  waiting for transfers between devices  141 us (52%)
  blocking collectives  43.6 us (16%)
  matrix products  31.4 us (12%)
  other arithmetic  18.1 us (7%)
  between operations  13.8 us (5%)
  local copies, waits for them, and re-layouts  9.79 us (4%)
  starting transfers between devices  7.77 us (3%)
    all_gather x1, waiting for transfers between devices, body(): own_weights = lax.all_gather(weights, CHIPS, axis=0, tiled=False)  75.7 us
    ppermute x1, waiting for transfers between devices, body(): from_left = lax.ppermute(learner_part, TP, to_right)  45.5 us
    all_to_all x1, blocking collectives, body(): lax.all_to_all(payload, SEQ, split_axis=0, concat_axis=0, tiled=True)  43.6 us
    dot_general x8, matrix products, body(): part = jnp.dot(cols, rows, preferred_element_type=jnp.float32)  19.5 us
    ppermute x3, waiting for transfers between devices, body(): lax.ppermute(own_sq, TP, [(t, (t + k) % tp_count) for t in range(tp_count)])  19.4 us
  transfers between devices with their start and end apart: 9, of which 4 were waited for; matrix products, arithmetic and copies ran while one was open for 11% of the time, Pallas kernels for 0%

profile of v4, /device:TPU:49, one launch (start us, length us, event | category | flops | bytes accessed | tf_op | source)
XLA Modules:
  0.0 265.0 jit_solution(12714974984477559538)
XLA Ops:
  6.5 2.1 pad_maximum_fusion.9
  8.7 0.0 all-gather.3.cloned.1.call-update
  8.7 0.7 add_select_fusion.3
  9.4 1.2 reduce-window.15
  10.6 0.2 slice_reduce_fusion
  10.8 0.1 fusion.79
  11.0 0.4 fusion.36
  11.4 0.1 copy.25
  11.5 3.1 %convolution_convert_fusion = bf16[32,20,2048]{2,0,1:T(8,128)(2,1)} fusion(bf16[512,2048]{1,0:T(8,128)(2,1)S(1)} %copy-done, pred[20,512]{1,0:T(8,128)(4,1)S(1)} %iota_compare_fusion.6, pred[32,512]{1,0:T(8,128)(4,1)S(1)} %iota_compare_fusion.5), kind=kOutput, calls=%fused_computation.24 | convolution fusion | flops 1343815680 | bytes 4745216 | tf_op jit(solution)/shard_map/psr,rf->psf/dot_general | solution.py:82
  14.6 75.7 %all-gather.3.cloned.1.call-done = bf16[4096,1280]{1,0:T(8,128)(2,1)} async-done(((bf16[256,1280]{1,0:T(8,128)(2,1)}), bf16[4096,1280]{1,0:T(8,128)(2,1)}) %all-gather.3.cloned.1.call-update) | async-done | bytes 10485776 | tf_op jit(solution)/shard_map/all_gather | solution.py:59
  90.3 0.8 collective-permute-start.3
  91.2 0.1 concatenate.58
  91.3 2.0 pad_maximum_fusion
  93.3 1.5 copy.29
  94.8 43.6 %all_to_all.5 = bf16[32,21,2048]{2,1,0:T(8,128)(2,1)S(1)} all-to-all(bf16[32,21,2048]{2,1,0:T(8,128)(2,1)S(1)} %copy.29), channel_id=1, replica_groups=mesh['chips'=16,'core'=2,'tp'=4] {'chips','core'}, dimensions={0} | all-to-all | bytes 5505024 | tf_op jit(solution)/shard_map/all_to_all | solution.py:89
  138.4 0.1 fusion.83
  138.5 0.1 copy.31
  138.6 4.0 %fusion.2 = (f32[512]{0:T(512)S(1)}, bf16[512,2048]{1,0:T(8,128)(2,1)}) fusion(bf16[32,20,2048]{2,1,0:T(8,128)(2,1)S(1)} %bitcast.106, s32[32,20]{0,1:T(8,128)S(1)} %copy.31), kind=kOutput, calls=%fused_computation.7 | convolution fusion | flops 1346698752 | bytes 4723200 | tf_op jit(solution)/shard_map/rps,psf->rf/dot_general | solution.py:94
  142.6 1.2 collective-permute-start.4
  143.8 1.5 collective-permute-start.5
  145.3 0.1 slice_compare_fusion
  145.3 0.1 add_select_fusion.4
  145.4 0.3 reduce-window.19
  145.7 0.1 slice.199
  145.8 0.1 slice_reduce_fusion.1
  146.0 45.5 %collective-permute-done.4 = bf16[512,2048]{1,0:T(8,128)(2,1)S(1)} collective-permute-done((bf16[512,2048]{1,0:T(8,128)(2,1)}, bf16[512,2048]{1,0:T(8,128)(2,1)S(1)}, u32[]{:S(2)}, u32[]{:S(2)}) %collective-permute-start.4) | collective-permute-done | bytes 2097184 | tf_op jit(solution)/shard_map/ppermute | solution.py:117
  191.4 1.1 slice.234
  192.5 0.1 collective-permute-start.6
  192.6 2.3 slice.235
  194.8 2.6 collective-permute-start.7
  197.4 0.1 fusion.88
  197.5 0.2 fusion.49
  197.7 1.8 multiply_cosine_fusion
  199.5 0.0 collective-permute-start
  199.6 1.3 collective-permute-start.1
  200.8 17.2 %collective-permute-done = f32[512]{0:T(512)S(1)} collective-permute-done((f32[512]{0:T(512)S(1)}, f32[512]{0:T(512)S(1)}, u32[]{:S(2)}, u32[]{:S(2)}) %collective-permute-start) | collective-permute-done | bytes 2080 | tf_op jit(solution)/shard_map/ppermute | solution.py:106
  218.1 0.3 collective-permute-start.2
  218.4 0.0 collective-permute-done.1
  218.4 2.1 collective-permute-done.2
  220.6 4.5 %multiply_convert_fusion.2 = (bf16[512,2048]{1,0:T(8,128)(2,1)S(1)}, bf16[512,2048]{1,0:T(8,128)(2,1)S(1)}, bf16[512,2048]{1,0:T(8,128)(2,1)S(1)}, bf16[512,2048]{1,0:T(8,128)(2,1)S(1)}) fusion(bf16[512,2048]{1,0:T(8,128)(2,1)S(1)} %collective-permute-done.4, f32[2048]{0:T(1024)S(1)} %get-tuple-element.43, f32[512]{0:T(512)S(1)} %add_rsqrt_fusion, ...), kind=kLoop, calls=%fused_computation.15 | loop fusion | flops 19922944 | bytes 16812032 | tf_op jit(solution)/shard_map/convert_element_type | solution.py:140
  225.1 0.4 fusion.110
  225.5 0.4 fusion.112
  226.0 0.8 slice-done.2
  226.8 1.6 fusion.20
  228.4 1.6 fusion.15
  229.9 1.6 fusion.12
  231.5 3.3 %convolution_add_fusion.4 = f32[512,1280]{1,0:T(8,128)S(1)} fusion(f32[512,1280]{1,0:T(8,128)S(1)} %fusion.20, bf16[4,1024,1280]{2,1,0:T(8,128)(2,1)} %bitcast.10, s32[]{:T(128)S(6)} %select_n.127, pred[]{:T(512)S(6)} %eq.108, bf16[512,256]{1,0:T(8,128)(2,1)S(1)} %get-tuple-element.67, bf16[512,256]{1,0:T(8,128)(2,1)S(1)} %get-tuple-element.66, ...), kind=kOutput, calls=%fused_computation.21 | convolution fusion | flops 1351745536 | bytes 9961477 | tf_op jit(solution)/shard_map/dot_general | solution.py:147
  234.8 1.6 convolution_add_fusion.3
  236.3 3.3 %fusion.8 = f32[512,1280]{1,0:T(8,128)S(1)} fusion(f32[512,1280]{1,0:T(8,128)S(1)} %fusion.15, f32[512,1280]{1,0:T(8,128)S(1)} %convolution_add_fusion.3, bf16[4,1024,1280]{2,1,0:T(8,128)(2,1)} %bitcast.10, s32[]{:T(128)S(6)} %select_n.132, pred[]{:T(512)S(6)} %eq.108, bf16[512,256]{1,0:T(8,128)(2,1)S(1)} %get-tuple-element.10, ...), kind=kOutput, calls=%fused_computation.22 | convolution fusion | flops 1352400896 | bytes 12582917 | tf_op jit(solution)/shard_map/dot_general | solution.py:147
  239.7 3.3 %fusion.9 = f32[512,1280]{1,0:T(8,128)S(1)} fusion(f32[512,1280]{1,0:T(8,128)S(1)} %fusion.12, f32[512,1280]{1,0:T(8,128)S(1)} %fusion.8, bf16[4,1024,1280]{2,1,0:T(8,128)(2,1)} %bitcast.10, s32[]{:T(128)S(6)} %select_n.137, pred[]{:T(512)S(6)} %eq.108, bf16[512,256]{1,0:T(8,128)(2,1)S(1)} %get-tuple-element.26, ...), kind=kOutput, calls=%fused_computation.23 | convolution fusion | flops 1352400896 | bytes 12582917 | tf_op jit(solution)/shard_map/dot_general | solution.py:147
  243.0 0.0 copy-start.6
  243.0 3.3 %convolution_add_fusion = f32[512,1280]{1,0:T(8,128)S(1)} fusion(f32[512,1280]{1,0:T(8,128)S(1)} %fusion.9, bf16[4,1024,1280]{2,1,0:T(8,128)(2,1)} %bitcast.10, s32[]{:T(128)S(6)} %select_n.142, pred[]{:T(512)S(6)} %eq.108, bf16[512,256]{1,0:T(8,128)(2,1)S(1)} %get-tuple-element.75, bf16[512,256]{1,0:T(8,128)(2,1)S(1)} %get-tuple-element.74, ...), kind=kOutput, calls=%fused_computation.17 | convolution fusion | flops 1351745536 | bytes 9961477 | tf_op jit(solution)/shard_map/dot_general | solution.py:147
  246.3 0.3 fusion.30
  246.6 0.5 copy.46
  247.1 0.0 copy-start.7
  247.1 0.7 fusion.109
  247.9 1.4 fusion.77
  249.3 0.8 subtract_convert_fusion
  250.2 2.2 fusion.1
  252.4 0.0 copy-start.8
  252.4 1.7 fusion
  254.1 0.0 copy-start.1
  254.1 2.7 %fusion.33 = bf16[128,8,512]{2,0,1:T(8,128)(2,1)S(1)} fusion(f32[8,512]{1,0:T(8,128)S(1)} %fusion, f32[8,512]{1,0:T(8,128)S(1)} %get-tuple-element.59, f32[512,512,8]{1,0,2:T(8,128)S(1)} %get-tuple-element.60, pred[512,512]{0,1:T(8,128)(4,1)S(1)} %fusion.49, f32[512,1280]{1,0:T(8,128)S(1)} %convolution_add_fusion, f32[128]{0:T(128)S(1)} %copy-done.8), kind=kOutput, calls=%fused_computation.53 | convolution fusion | flops 548012032 | bytes 9994752 | tf_op jit(solution)/shard_map/kgqp,pkd->qkgd/dot_general | solution.py:176
  256.8 1.3 copy.37
  (39 shorter events, 0.3 us)
Async XLA Ops:
  6.5 5.0 %copy-start = (bf16[512,2048]{1,0:T(8,128)(2,1)S(1)}, bf16[512,2048]{1,0:T(8,128)(2,1)}, u32[]{:S(2)}) copy-start(bf16[512,2048]{1,0:T(8,128)(2,1)} %param.10) | copy-start | bytes 6291460
  6.5 83.7 %all-gather.3.cloned.1.call-start = ((), (), s32[]{:S(2)}) async-start(), calls=%async_computation.1 | async-start | bytes 11141120 | tf_op jit(solution)/shard_map/all_gather | solution.py:59
  90.3 141.2 %collective-permute-start.3 = (bf16[16,256,1280]{2,1,0:T(8,128)(2,1)}, bf16[16,256,1280]{2,1,0:T(8,128)(2,1)}, u32[]{:S(2)}, u32[]{:S(2)}) collective-permute-start(bf16[16,256,1280]{2,1,0:T(8,128)(2,1)} %bitcast.110), channel_id=1, source_target_pairs={{0,4},{4,0},{1,5},{5,1},{2,6},{6,2},{3,7},{7,3},{8,12},{12,8},{9,1... | collective-permute-start | bytes 31457288 | tf_op jit(solution)/shard_map/ppermute | solution.py:60
  138.6 6.7 %copy-start.4 = (s32[512]{0:T(512)S(1)}, s32[512]{0:T(512)}, u32[]{:S(2)}) copy-start(s32[512]{0:T(512)} %param.12) | copy-start | bytes 6148
  142.6 48.8 %collective-permute-start.4 = (bf16[512,2048]{1,0:T(8,128)(2,1)}, bf16[512,2048]{1,0:T(8,128)(2,1)S(1)}, u32[]{:S(2)}, u32[]{:S(2)}) collective-permute-start(bf16[512,2048]{1,0:T(8,128)(2,1)} %get-tuple-element.58), channel_id=1, source_target_pairs={{0,1},{1,2},{2,3},{3,0},{4,5},{5,6},{6,7},{7,4},{8,9},{9,10},{10,1... | collective-permute-start | bytes 6291464 | tf_op jit(solution)/shard_map/ppermute | solution.py:117
  143.8 48.8 %collective-permute-start.5 = (bf16[512,2048]{1,0:T(8,128)(2,1)}, bf16[512,2048]{1,0:T(8,128)(2,1)}, u32[]{:S(2)}, u32[]{:S(2)}) collective-permute-start(bf16[512,2048]{1,0:T(8,128)(2,1)} %get-tuple-element.58), channel_id=1, source_target_pairs={{0,3},{1,0},{2,1},{3,2},{4,7},{5,4},{6,5},{7,6},{8,11},{9,8},{10,9... | collective-permute-start | bytes 6291464 | tf_op jit(solution)/shard_map/ppermute | solution.py:118
  146.0 72.4 %copy-start.5 = (f32[8192]{0:T(1024)S(1)}, f32[8192]{0:T(1024)}, u32[]{:S(2)}) copy-start(f32[8192]{0:T(1024)} %param.13) | copy-start | bytes 98308
  192.5 28.0 %collective-permute-start.6 = (bf16[512,1024]{1,0:T(8,128)(2,1)}, bf16[512,1024]{1,0:T(8,128)(2,1)S(1)}, u32[]{:S(2)}, u32[]{:S(2)}) collective-permute-start(bf16[512,1024]{1,0:T(8,128)(2,1)} %slice.234), channel_id=1, source_target_pairs={{0,1},{1,2},{2,3},{3,0},{4,5},{5,6},{6,7},{7,4},{8,9},{9,10},{10,1... | collective-permute-start | bytes 3145736 | tf_op jit(solution)/shard_map/ppermute | solution.py:119
  194.8 25.7 %collective-permute-start.7 = (bf16[512,1024]{1,0:T(8,128)(2,1)}, bf16[512,1024]{1,0:T(8,128)(2,1)}, u32[]{:S(2)}, u32[]{:S(2)}) collective-permute-start(bf16[512,1024]{1,0:T(8,128)(2,1)} %slice.235), channel_id=1, source_target_pairs={{0,3},{1,0},{2,1},{3,2},{4,7},{5,4},{6,5},{7,6},{8,11},{9,8},{10,9... | collective-permute-start | bytes 3145736 | tf_op jit(solution)/shard_map/ppermute | solution.py:120
  199.5 18.5 %collective-permute-start = (f32[512]{0:T(512)S(1)}, f32[512]{0:T(512)S(1)}, u32[]{:S(2)}, u32[]{:S(2)}) collective-permute-start(f32[512]{0:T(512)S(1)} %get-tuple-element.57), channel_id=1, source_target_pairs={{0,1},{1,2},{2,3},{3,0},{4,5},{5,6},{6,7},{7,4},{8,9},{9,10},{10,1... | collective-permute-start | bytes 6152 | tf_op jit(solution)/shard_map/ppermute | solution.py:106
  199.6 18.8 %collective-permute-start.1 = (f32[512]{0:T(512)S(1)}, f32[512]{0:T(512)S(1)}, u32[]{:S(2)}, u32[]{:S(2)}) collective-permute-start(f32[512]{0:T(512)S(1)} %get-tuple-element.57), channel_id=1, source_target_pairs={{0,2},{1,3},{2,0},{3,1},{4,6},{5,7},{6,4},{7,5},{8,10},{9,11},{10,... | collective-permute-start | bytes 6152 | tf_op jit(solution)/shard_map/ppermute | solution.py:106
  218.1 2.4 collective-permute-start.2
  220.5 5.4 %slice-start = ((s8[10485760]{0:T(1024)(128)(4,1)}), s8[4194304]{0:T(1024)(128)(4,1)S(1)}, s32[]{:S(2)}) async-start(s8[10485760]{0:T(1024)(128)(4,1)} %bitcast.111), calls=%async_computation.2 | async-start | bytes 8388608
  220.5 5.4 %slice-start.1 = ((s8[10485760]{0:T(1024)(128)(4,1)}), s8[4194304]{0:T(1024)(128)(4,1)S(1)}, s32[]{:S(2)}) async-start(s8[10485760]{0:T(1024)(128)(4,1)} %bitcast.111), calls=%async_computation.3 | async-start | bytes 8388608
  225.1 1.7 slice-start.2
  243.0 3.3 %copy-start.6 = (f32[1024]{0:T(1024)S(1)}, f32[1024]{0:T(1024)}, u32[]{:S(2)}) copy-start(f32[1024]{0:T(1024)} %param.17) | copy-start | bytes 12292
  247.1 0.7 copy-start.7
  247.1 2.2 copy-start.2
  247.1 2.2 copy-start.3
  252.4 1.8 copy-start.8
  254.1 4.0 %copy-start.1 = (bf16[512,2048]{1,0:T(8,128)(2,1)S(1)}, bf16[512,2048]{1,0:T(8,128)(2,1)}, u32[]{:S(2)}) copy-start(bf16[512,2048]{1,0:T(8,128)(2,1)} %param.10) | copy-start | bytes 6291460
Sparse Core Ops, SparseCore 0:
  9.5 80.7 all-gather.2
